TPU v7x, 128 devices: a whole 4x4x4 slice. The times are simulated.
128 devices in a mesh: bx: 8 (over z, core), by: 16 (over x, y).
Axes of the slice: x: 4, y: 4, z: 4, core: 2. Of those that a mesh axis runs over, the one named last changes fastest.
Arguments:
- adjoint_source: float32 [5, 32, 64, 512], P(None, 'bx', 'by'), may hold values from -5 to 5
- initial: float32 [5, 32, 64, 512], P(None, 'bx', 'by'), may hold values from -6 to 6
- inverses: float32 [5, 5, 32, 64, 512], P(None, None, 'bx', 'by'), may hold values from -0.23 to 0.48
- couplings: bfloat16 [6, 5, 5, 32, 64, 512], P(None, None, None, 'bx', 'by'), may hold values from -3.7 to 1.3
- interface_tiles: float32 [128, 5, 5, 256], P(('bx', 'by')), may hold values from -2.5 to 2.5
- source_cells: int32 [128, 256], P(('bx', 'by')), may hold values from 0 to 8191
- target_cells: int32 [128, 256], P(('bx', 'by')), may hold values from 0 to 8191
- tile_counts: int32 [128, 128], P(('bx', 'by')), may hold values from 1 to 2, as said below
Outputs:
- adjoint: float32 [5, 32, 64, 512], P(None, 'bx', 'by')
Inputs may be any that keep to these rules, and one draw needn't show every extreme that they name: Slots k of the group of receiving block d with k < tile_counts[o, d] hold tiles; the others are padding. In every draw one receiving block gets 2 tiles from every block.
All inputs are finite; a program needn't handle non-finite values.
Results may differ from a plain program's by a relative error of at most 0.0003.
Values sent between devices are 32-bit elements; how exact they have to be, the bound alone decides.
No kernel may reach another device: no remote copies, remote signals or barrier semaphores. Data moves between devices by JAX's collectives and lax.ppermute only.
A program may use at most 64 MiB of HBM per device.

v0:
```python
import jax
import jax.numpy as jnp
from jax import lax
from jax.sharding import PartitionSpec as P

ITERS = 2


def shifted(block, axis, distance):
    devices = range(lax.axis_size(axis))
    route = [(i - distance, i) for i in devices if i - distance in devices]
    return lax.ppermute(block, axis, route)


def matvec(matrix, vector):
    return jnp.sum(matrix.astype(jnp.float32) * vector[None], axis=1)


def neighbour(values, axis_at, offset):
    length = values.shape[axis_at]
    border = jnp.zeros_like(lax.slice_in_dim(values, 0, 1, axis=axis_at))
    if offset > 0:
        return jnp.concatenate(
            [lax.slice_in_dim(values, 1, length, axis=axis_at), border], axis=axis_at
        )
    return jnp.concatenate(
        [border, lax.slice_in_dim(values, 0, length - 1, axis=axis_at)], axis=axis_at
    )


def send_faces(across_x, across_y, offset):
    return (shifted(across_x, "bx", offset), shifted(across_y, "by", offset))


def solve_block(fixed, inverses, along_x, along_y, inflow_x, inflow_y, forward):
    count_x = fixed.shape[1]
    count_y = fixed.shape[2]
    order_x = list(range(count_x)) if forward else list(reversed(range(count_x)))
    order_y = list(range(count_y)) if forward else list(reversed(range(count_y)))
    offset = -1 if forward else 1
    finished = {}
    for x in order_x:
        for y in order_y:
            from_x = finished[x + offset, y] if (x + offset, y) in finished else inflow_x[:, y]
            from_y = finished[x, y + offset] if (x, y + offset) in finished else inflow_y[:, x]
            right = (
                fixed[:, x, y]
                - matvec(along_x[:, :, x, y], from_x)
                - matvec(along_y[:, :, x, y], from_y)
            )
            finished[x, y] = matvec(inverses[:, :, x, y], right)
    planes = [jnp.stack([finished[x, y] for y in range(count_y)], axis=1) for x in range(count_x)]
    return jnp.stack(planes, axis=1)


def wavefront(fixed, inverses, along_x, along_y, forward, pieces):
    count_x = fixed.shape[1]
    count_y = fixed.shape[2]
    width = fixed.shape[3] // pieces
    offset = 1 if forward else -1
    if forward:
        my_turn = lax.axis_index("bx") + lax.axis_index("by")
    else:
        my_turn = (
            lax.axis_size("bx")
            - 1
            - lax.axis_index("bx")
            + (lax.axis_size("by") - 1 - lax.axis_index("by"))
        )
    total = lax.axis_size("bx") + lax.axis_size("by") - 2 + pieces
    edge_x = count_x - 1 if forward else 0
    edge_y = count_y - 1 if forward else 0
    start_x = jnp.zeros((fixed.shape[0], count_y, width), jnp.float32)
    start_y = jnp.zeros((fixed.shape[0], count_x, width), jnp.float32)

    def advance(t, carry):
        result, out_x, out_y = carry
        inflow_x, inflow_y = send_faces(out_x, out_y, offset)
        piece = t - my_turn

        def active():
            first = jnp.clip(piece, 0, pieces - 1).astype(jnp.int32) * width

            def slab_of(source):
                return lax.dynamic_slice_in_dim(source, first, width, axis=source.ndim - 1)

            block = solve_block(
                slab_of(fixed),
                slab_of(inverses),
                slab_of(along_x),
                slab_of(along_y),
                inflow_x,
                inflow_y,
                forward,
            )
            return (
                lax.dynamic_update_slice_in_dim(result, block, first, axis=3),
                block[:, edge_x],
                block[:, :, edge_y],
            )

        def resting():
            return (result, out_x, out_y)

        return lax.cond((piece >= 0) & (piece < pieces), active, resting)

    result, out_x, out_y = lax.fori_loop(
        0, total, advance, (jnp.zeros_like(fixed), start_x, start_y)
    )
    return result


def interface(iterate, interface_tiles, source_cells, target_cells, tile_counts):
    var_count = iterate.shape[0]
    flat_cells = iterate.reshape(var_count, -1)
    block_count = lax.axis_size("bx") * lax.axis_size("by")
    slot_count = source_cells.shape[1]
    per_pair = slot_count // block_count
    picked = jnp.take(flat_cells, source_cells[0], axis=1)
    products = jnp.sum(interface_tiles[0] * picked[None], axis=1)
    slot_ids = jnp.arange(slot_count, dtype=jnp.int32)
    limits = jnp.repeat(tile_counts[0], per_pair)
    products = jnp.where((slot_ids % per_pair)[None] < limits[None], products, 0.0)
    arrived = lax.all_to_all(products, ("bx", "by"), split_axis=1, concat_axis=1, tiled=True)
    summed = jnp.zeros_like(flat_cells).at[:, target_cells[0]].add(arrived)
    return summed.reshape(iterate.shape)


def per_device(
    adjoint_source,
    initial,
    inverses,
    couplings,
    interface_tiles,
    source_cells,
    target_cells,
    tile_counts,
):
    pieces = 1
    iterate = initial
    for number in range(ITERS):
        inter = interface(iterate, interface_tiles, source_cells, target_cells, tile_counts)
        base = adjoint_source - inter
        rim_x, rim_y = send_faces(iterate[:, 0], iterate[:, :, 0], -1)
        above_x = jnp.concatenate([iterate[:, 1:], rim_x[:, None]], axis=1)
        above_y = jnp.concatenate([iterate[:, :, 1:], rim_y[:, :, None]], axis=2)
        lower_terms = (
            base
            - matvec(couplings[1], above_x)
            - matvec(couplings[3], above_y)
            - matvec(couplings[4], neighbour(iterate, 3, -1))
            - matvec(couplings[5], neighbour(iterate, 3, 1))
        )
        half = wavefront(lower_terms, inverses, couplings[0], couplings[2], True, pieces)
        rim_x, rim_y = send_faces(half[:, -1], half[:, :, -1], 1)
        below_x = jnp.concatenate([rim_x[:, None], half[:, :-1]], axis=1)
        below_y = jnp.concatenate([rim_y[:, :, None], half[:, :, :-1]], axis=2)
        upper_terms = (
            base
            - matvec(couplings[0], below_x)
            - matvec(couplings[2], below_y)
            - matvec(couplings[4], neighbour(half, 3, -1))
            - matvec(couplings[5], neighbour(half, 3, 1))
        )
        iterate = wavefront(upper_terms, inverses, couplings[1], couplings[3], False, pieces)
    return iterate


def solution(mesh):
    return jax.shard_map(
        per_device,
        mesh=mesh,
        in_specs=(
            P(None, "bx", "by", None),
            P(None, "bx", "by", None),
            P(None, None, "bx", "by", None),
            P(None, None, None, "bx", "by", None),
            P(("bx", "by"), None, None, None),
            P(("bx", "by"), None),
            P(("bx", "by"), None),
            P(("bx", "by"), None),
        ),
        out_specs=P(None, "bx", "by", None),
        check_vma=False,
    )
```

profile of v0, /device:TPU:1, one launch (start us, length us, event | category | flops | bytes accessed | tf_op | source)
XLA Modules:
  0.0 1218.1 jit_solution(9217197256090378448)
XLA Ops:
  9.3 11.9 all-to-all-start
  45.4 243.8 %while.68 = (s32[]{:T(128)}, f32[5,4,4,512]{3,0,2,1:T(8,128)}, f32[5,4,512]{2,0,1:T(8,128)}, f32[5,4,512]{2,0,1:T(8,128)}, s32[]{:T(128)}, /*index=5*/f32[5,5,4,...) while((s32[]{:T(128)}, f32[5,4,4,512]{3,0,2,1:T(8,128)}, ...), condition=%wide.region_57.59_spmd, body=%wide.region_6.58_spmd.sunk | while | flops 1873927 | bytes 7762251 | solution.py:107
  74.0 8.9 collective-permute-start
  89.4 8.9 collective-permute-start.1
  112.1 6.6 collective-permute-start.1
  132.5 7.1 collective-permute-start.1
  153.4 8.2 collective-permute-start.1
  176.4 6.1 collective-permute-start.1
  186.9 6.1 collective-permute-start.1
  207.8 6.1 collective-permute-start.1
  218.3 6.1 collective-permute-start.1
  239.2 6.1 collective-permute-start.1
  260.1 6.1 collective-permute-start.1
  270.6 6.1 collective-permute-start.1
  296.7 6.3 collective-permute-start.11
  306.7 298.9 %while.69 = (s32[]{:T(128)}, f32[5,4,4,512]{3,0,2,1:T(8,128)}, f32[5,4,512]{2,0,1:T(8,128)S(1)}, f32[5,4,512]{2,0,1:T(8,128)S(1)}, s32[]{:T(128)}, /*index=5*/f3...) while((s32[]{:T(128)}, f32[5,4,4,512]{3,0,2,1:T(8,128)}, ...), condition=%wide.region_113.115_spmd, body=%wide.region_62.114_spmd.sunk | while | flops 1873927 | bytes 7762251 | solution.py:107
  371.6 6.4 collective-permute-done.2
  381.7 7.0 collective-permute-done.2
  391.9 7.9 collective-permute-done.2
  403.0 7.8 collective-permute-done.2
  414.1 7.8 collective-permute-done.2
  425.2 7.6 collective-permute-done.2
  436.0 7.9 collective-permute-done.2
  447.1 7.2 collective-permute-done.2
  457.6 7.2 collective-permute-done.2
  468.0 7.2 collective-permute-done.2
  478.4 7.2 collective-permute-done.2
  488.8 7.2 collective-permute-done.2
  499.2 7.2 collective-permute-done.2
  509.6 7.2 collective-permute-done.2
  528.7 65.2 %collective-permute-done.2 = f32[5,4,512]{2,0,1:T(8,128)S(1)} collective-permute-done((f32[5,4,512]{2,0,1:T(8,128)S(1)}, f32[5,4,512]{2,0,1:T(8,128)S(1)}, u32[]{:S(2)}, u32[]{:S(2)}) %collective-permute-start.2) | collective-permute-done | bytes 40992 | tf_op jit(solution)/shard_map/while/body/eval_jaxpr/ppermute | solution.py:12
  620.5 10.1 all-to-all-start.1
  656.1 243.8 %while.70 = (s32[]{:T(128)}, f32[5,4,4,512]{3,0,2,1:T(8,128)}, f32[5,4,512]{2,0,1:T(8,128)}, f32[5,4,512]{2,0,1:T(8,128)}, s32[]{:T(128)}, /*index=5*/f32[5,5,4,...) while((s32[]{:T(128)}, f32[5,4,4,512]{3,0,2,1:T(8,128)}, ...), condition=%wide.region_171.173_spmd, body=%wide.region_120.172_spmd.sunk | while | flops 1873927 | bytes 7762251 | solution.py:107
  684.7 8.9 collective-permute-start.4
  700.1 8.9 collective-permute-start.5
  722.8 6.6 collective-permute-start.5
  743.2 7.1 collective-permute-start.5
  764.1 8.2 collective-permute-start.5
  787.1 6.1 collective-permute-start.5
  797.7 6.1 collective-permute-start.5
  818.6 6.1 collective-permute-start.5
  829.1 6.1 collective-permute-start.5
  870.8 6.1 collective-permute-start.5
  881.3 6.1 collective-permute-start.5
  902.0 6.1 collective-permute-start.15
  917.1 299.4 %while.71 = (s32[]{:T(128)}, f32[5,4,4,512]{3,0,2,1:T(8,128)}, f32[5,4,512]{2,0,1:T(8,128)S(1)}, f32[5,4,512]{2,0,1:T(8,128)S(1)}, s32[]{:T(128)}, /*index=5*/f3...) while((s32[]{:T(128)}, f32[5,4,4,512]{3,0,2,1:T(8,128)}, ...), condition=%wide.region_227.229_spmd, body=%wide.region_176.228_spmd.sunk | while | flops 1873927 | bytes 7762251 | solution.py:107
  949.4 6.8 collective-permute-done.6
  959.5 7.7 collective-permute-done.6
  970.4 7.9 collective-permute-done.6
  981.5 7.8 collective-permute-done.6
  992.6 7.7 collective-permute-done.6
  1003.5 7.8 collective-permute-done.6
  1014.5 7.8 collective-permute-done.6
  1025.6 7.7 collective-permute-done.6
  1036.5 7.7 collective-permute-done.6
  1047.5 7.2 collective-permute-done.6
  1057.9 7.2 collective-permute-done.6
  1068.3 7.2 collective-permute-done.6
  1078.7 7.2 collective-permute-done.6
  1089.1 7.2 collective-permute-done.6
  1099.5 7.2 collective-permute-done.6
  1110.0 7.2 collective-permute-done.6
  1120.4 7.2 collective-permute-done.6
  1139.4 65.3 %collective-permute-done.6 = f32[5,4,512]{2,0,1:T(8,128)S(1)} collective-permute-done((f32[5,4,512]{2,0,1:T(8,128)S(1)}, f32[5,4,512]{2,0,1:T(8,128)S(1)}, u32[]{:S(2)}, u32[]{:S(2)}) %collective-permute-start.6) | collective-permute-done | bytes 40992 | tf_op jit(solution)/shard_map/while/body/eval_jaxpr/ppermute | solution.py:12
  (822 shorter events, 681.8 us)
Async XLA Ops:
  9.3 22.3 %all-to-all-start = ((f32[5,128,2]{0,2,1:T(2,128)}), f32[5,128,2]{0,2,1:T(2,128)}, u32[]{:S(2)}, u32[]{:S(2)}) async-start(f32[5,128,2]{0,2,1:T(2,128)} %broadcast_select_fusion.1), calls=%async_computation | async-start | bytes 262144 | tf_op jit(solution)/shard_map/all_to_all | solution.py:124
  21.9 17.2 %collective-permute-start.9 = (f32[5,4,512]{2,1,0:T(4,128)}, f32[5,4,512]{2,1,0:T(4,128)}, u32[]{:S(2)}, u32[]{:S(2)}) collective-permute-start(f32[5,4,512]{2,1,0:T(4,128)} %bitcast.1264), channel_id=1, source_target_pairs={{1,0},{2,1},{3,2},{4,3},{5,4},{6,5},{7,6},{8,7},{9,8},{10,9},{11,1... | collective-permute-start | bytes 122888 | tf_op jit(solution)/shard_map/ppermute | solution.py:12
  23.2 17.7 %collective-permute-start.8 = (f32[5,4,512]{2,1,0:T(4,128)S(1)}, f32[5,4,512]{2,1,0:T(4,128)S(1)}, u32[]{:S(2)}, u32[]{:S(2)}) collective-permute-start(f32[5,4,512]{2,1,0:T(4,128)S(1)} %slice_bitcast_fusion.80), channel_id=1, source_target_pairs={{16,0},{32,16},{48,32},{64,48},{80,64},{96,80},{112,96},{17,1},{33... | collective-permute-start | bytes 122888 | tf_op jit(solution)/shard_map/ppermute | solution.py:12
  74.0 11.8 collective-permute-start
  87.5 10.9 collective-permute-start
  89.4 10.6 collective-permute-start.1
  108.6 10.1 collective-permute-start
  129.9 9.7 collective-permute-start
  132.5 9.2 collective-permute-start.1
  150.5 11.2 collective-permute-start
  153.4 10.3 collective-permute-start.1
  291.3 11.9 collective-permute-start.10
  368.1 9.9 collective-permute-start.2
  378.2 10.4 collective-permute-start.2
  388.6 11.2 collective-permute-start.2
  390.6 9.2 collective-permute-start.3
  399.8 11.1 collective-permute-start.2
  401.7 9.1 collective-permute-start.3
  410.9 11.1 collective-permute-start.2
  421.9 10.8 collective-permute-start.2
  432.8 11.2 collective-permute-start.2
  434.7 9.2 collective-permute-start.3
  443.9 10.4 collective-permute-start.2
  454.3 10.4 collective-permute-start.2
  464.7 10.4 collective-permute-start.2
  475.2 10.4 collective-permute-start.2
  485.6 10.4 collective-permute-start.2
  496.0 10.4 collective-permute-start.2
  506.4 10.4 collective-permute-start.2
  525.5 68.4 %collective-permute-start.2 = (f32[5,4,512]{2,0,1:T(8,128)S(1)}, f32[5,4,512]{2,0,1:T(8,128)S(1)}, u32[]{:S(2)}, u32[]{:S(2)}) collective-permute-start(f32[5,4,512]{2,0,1:T(8,128)S(1)} %get-tuple-element.1546), channel_id=1, source_target_pairs={{16,0},{32,16},{48,32},{64,48},{80,64},{96,80},{112,96},{17,1},{33... | collective-permute-start | bytes 122888 | tf_op jit(solution)/shard_map/while/body/eval_jaxpr/ppermute | solution.py:12
  527.4 66.5 %collective-permute-start.3 = (f32[5,4,512]{2,0,1:T(8,128)S(1)}, f32[5,4,512]{2,0,1:T(8,128)S(1)}, u32[]{:S(2)}, u32[]{:S(2)}) collective-permute-start(f32[5,4,512]{2,0,1:T(8,128)S(1)} %get-tuple-element.1547), channel_id=1, source_target_pairs={{1,0},{2,1},{3,2},{4,3},{5,4},{6,5},{7,6},{8,7},{9,8},{10,9},{11,1... | collective-permute-start | bytes 122888 | tf_op jit(solution)/shard_map/while/body/eval_jaxpr/ppermute | solution.py:12
  620.5 21.0 %all-to-all-start.1 = ((f32[5,128,2]{0,2,1:T(2,128)}), f32[5,128,2]{0,2,1:T(2,128)}, u32[]{:S(2)}, u32[]{:S(2)}) async-start(f32[5,128,2]{0,2,1:T(2,128)} %broadcast_select_fusion), calls=%async_computation.1 | async-start | bytes 262144 | tf_op jit(solution)/shard_map/all_to_all | solution.py:124
  630.6 18.3 %collective-permute-start.13 = (f32[5,4,512]{2,0,1:T(8,128)}, f32[5,4,512]{2,0,1:T(8,128)}, u32[]{:S(2)}, u32[]{:S(2)}) collective-permute-start(f32[5,4,512]{2,0,1:T(8,128)} %slice_bitcast_fusion.77), channel_id=1, source_target_pairs={{1,0},{2,1},{3,2},{4,3},{5,4},{6,5},{7,6},{8,7},{9,8},{10,9},{11,1... | collective-permute-start | bytes 122888 | tf_op jit(solution)/shard_map/ppermute | solution.py:12
  636.9 13.8 %collective-permute-start.12 = (f32[5,4,512]{2,0,1:T(8,128)}, f32[5,4,512]{2,0,1:T(8,128)}, u32[]{:S(2)}, u32[]{:S(2)}) collective-permute-start(f32[5,4,512]{2,0,1:T(8,128)} %slice_bitcast_fusion.78), channel_id=1, source_target_pairs={{16,0},{32,16},{48,32},{64,48},{80,64},{96,80},{112,96},{17,1},{33... | collective-permute-start | bytes 122888 | tf_op jit(solution)/shard_map/ppermute | solution.py:12
  684.7 11.8 collective-permute-start.4
  698.2 10.9 collective-permute-start.4
  700.1 10.6 collective-permute-start.5
  719.3 10.1 collective-permute-start.4
  740.6 9.7 collective-permute-start.4
  743.2 9.2 collective-permute-start.5
  761.3 11.0 collective-permute-start.4
  764.1 10.3 collective-permute-start.5
  902.0 12.0 collective-permute-start.15
  936.3 9.3 collective-permute-start.6
  946.1 10.2 collective-permute-start.6
  956.2 10.9 collective-permute-start.6
  967.2 11.1 collective-permute-start.6
  969.1 9.2 collective-permute-start.7
  978.3 11.1 collective-permute-start.6
  989.3 10.9 collective-permute-start.6
  1000.3 11.0 collective-permute-start.6
  1011.3 11.1 collective-permute-start.6
  1022.4 10.9 collective-permute-start.6
  1033.3 10.9 collective-permute-start.6
  1044.2 10.4 collective-permute-start.6
  1054.6 10.4 collective-permute-start.6
  1065.1 10.4 collective-permute-start.6
  1075.5 10.4 collective-permute-start.6
  1085.9 10.4 collective-permute-start.6
  1096.3 10.4 collective-permute-start.6
  1106.7 10.4 collective-permute-start.6
  1117.1 10.4 collective-permute-start.6
  1136.2 68.5 %collective-permute-start.6 = (f32[5,4,512]{2,0,1:T(8,128)S(1)}, f32[5,4,512]{2,0,1:T(8,128)S(1)}, u32[]{:S(2)}, u32[]{:S(2)}) collective-permute-start(f32[5,4,512]{2,0,1:T(8,128)S(1)} %get-tuple-element.1612), channel_id=1, source_target_pairs={{16,0},{32,16},{48,32},{64,48},{80,64},{96,80},{112,96},{17,1},{33... | collective-permute-start | bytes 122888 | tf_op jit(solution)/shard_map/while/body/eval_jaxpr/ppermute | solution.py:12
  1138.1 66.6 %collective-permute-start.7 = (f32[5,4,512]{2,0,1:T(8,128)S(1)}, f32[5,4,512]{2,0,1:T(8,128)S(1)}, u32[]{:S(2)}, u32[]{:S(2)}) collective-permute-start(f32[5,4,512]{2,0,1:T(8,128)S(1)} %get-tuple-element.1613), channel_id=1, source_target_pairs={{1,0},{2,1},{3,2},{4,3},{5,4},{6,5},{7,6},{8,7},{9,8},{10,9},{11,1... | collective-permute-start | bytes 122888 | tf_op jit(solution)/shard_map/while/body/eval_jaxpr/ppermute | solution.py:12
  (155 other events, 1194.8 us)
where the time goes:
time: 1230 us; the launch traced here: 1220 us
  starting transfers between devices  586 us (48%)
  waiting for transfers between devices  525 us (43%)
  local copies, waits for them, and re-layouts  64.9 us (5%)
  other arithmetic  37.1 us (3%)
    ppermute x192, starting transfers between devices, shifted(): return lax.ppermute(block, axis, route)  564 us
    ppermute x192, waiting for transfers between devices, shifted(): return lax.ppermute(block, axis, route)  525 us
  transfers between devices with their start and end apart: 194, of which 108 were waited for; matrix products, arithmetic and copies ran while one was open for 3% of the time, Pallas kernels for 0%

commit v1 on v0

v1 whole, which is shorter than its diff:
```python
import functools

import jax
import jax.numpy as jnp
from jax import lax
from jax.experimental import pallas as pl
from jax.experimental.pallas import tpu as pltpu
from jax.sharding import PartitionSpec as P

ITERS = 2
AXES = ("bx", "by")
ROWS = 8


def interface(iterate, interface_tiles, source_cells, target_cells, tile_counts):
    var_count = iterate.shape[0]
    flat_cells = iterate.reshape(var_count, -1)
    block_count = lax.axis_size("bx") * lax.axis_size("by")
    slot_count = source_cells.shape[1]
    per_pair = slot_count // block_count
    picked = jnp.take(flat_cells, source_cells[0], axis=1)
    products = jnp.sum(interface_tiles[0] * picked[None], axis=1)
    slot_ids = jnp.arange(slot_count, dtype=jnp.int32)
    limits = jnp.repeat(tile_counts[0], per_pair)
    products = jnp.where((slot_ids % per_pair)[None] < limits[None], products, 0.0)
    arrived = lax.all_to_all(products, AXES, split_axis=1, concat_axis=1, tiled=True)
    summed = jnp.zeros_like(flat_cells).at[:, target_cells[0]].add(arrived)
    return summed.reshape(iterate.shape)


def to_slices(values, devices):
    count, ca, cb, nz = values.shape
    shaped = jnp.transpose(values, (3, 1, 2, 0))
    return shaped.reshape(devices, (nz // devices) * ca * cb, count)


def gather_grid(received, n_bx, n_by, ca, cb, width):
    count = received.shape[2]
    shaped = received.reshape(n_bx, n_by, width, ca, cb, count)
    shaped = jnp.transpose(shaped, (1, 4, 5, 2, 0, 3))
    return shaped.reshape(n_by * cb, count, width * n_bx * ca)


def scatter_grid(grid, n_bx, n_by, ca, cb, width):
    ny, count, lanes = grid.shape
    shaped = grid.reshape(n_by, cb, count, width, n_bx, ca)
    shaped = jnp.transpose(shaped, (4, 0, 3, 5, 1, 2))
    return shaped.reshape(n_bx * n_by, width * ca * cb, count)


def from_slices(received, ca, cb):
    src, rows, count = received.shape
    width = rows // (ca * cb)
    shaped = received.reshape(src * width, ca, cb, count)
    return jnp.transpose(shaped, (3, 1, 2, 0))


def lane_x(shape, nx):
    return lax.broadcasted_iota(jnp.int32, shape, len(shape) - 1) % nx


def skew(grid, steps, nx):
    ny = grid.shape[0]
    values = jnp.pad(grid, ((0, steps - ny), (0, 0), (0, 0)))
    x = lane_x(values.shape, nx)
    bit = 1
    while bit < nx:
        values = lax.optimization_barrier(values)
        moved = jnp.concatenate([jnp.zeros_like(values[:bit]), values[:-bit]], axis=0)
        values = jnp.where((x & bit) != 0, moved, values)
        bit *= 2
    return values


def unskew(values, ny, nx):
    x = lane_x(values.shape, nx)
    bit = 1
    while bit < nx:
        values = lax.optimization_barrier(values)
        moved = jnp.concatenate([values[bit:], jnp.zeros_like(values[:bit])], axis=0)
        values = jnp.where((x & bit) != 0, moved, values)
        bit *= 2
    return values[:ny]


def as_vectors(rows):
    return jnp.pad(rows, ((0, 0), (0, ROWS - rows.shape[1]), (0, 0)))


def as_matrices(rows, count):
    steps, _, lanes = rows.shape
    shaped = rows.reshape(steps, count, count, lanes)
    return jnp.pad(shaped, ((0, 0), (0, 0), (0, ROWS - count), (0, 0)))


def matvec(matrix, vector):
    count = matrix.shape[1]
    return jnp.sum(matrix * vector[:, :count, None, :], axis=1)


def shift_t(values, offset):
    zero = jnp.zeros_like(values[:1])
    if offset > 0:
        return jnp.concatenate([values[1:], zero], axis=0)
    return jnp.concatenate([zero, values[:-1]], axis=0)


def shift_x(values, offset, nx):
    x = lane_x(values.shape, nx)
    zero = jnp.zeros_like(values[..., :1])
    if offset > 0:
        moved = jnp.concatenate([values[..., 1:], zero], axis=-1)
        return jnp.where(x == nx - 1, 0.0, moved)
    moved = jnp.concatenate([zero, values[..., :-1]], axis=-1)
    return jnp.where(x == 0, 0.0, moved)


def shift_z(values, offset, nx, devices, count):
    rows = values.shape[1]
    if offset > 0:
        halo = lax.ppermute(values[:, :count, :nx], AXES, [(i + 1, i) for i in range(devices - 1)])
        halo = jnp.pad(halo, ((0, 0), (0, rows - count), (0, 0)))
        return jnp.concatenate([values[..., nx:], halo], axis=-1)
    halo = lax.ppermute(values[:, :count, -nx:], AXES, [(i, i + 1) for i in range(devices - 1)])
    halo = jnp.pad(halo, ((0, 0), (0, rows - count), (0, 0)))
    return jnp.concatenate([halo, values[..., :-nx]], axis=-1)


def sweep_kernel(rhs_ref, kx_ref, ky_ref, inv_ref, out_ref, *, forward, nx, count):
    steps = rhs_ref.shape[0]
    lanes = rhs_ref.shape[2]
    x = lax.broadcasted_iota(jnp.int32, (ROWS, lanes), 1) % nx
    if forward:
        keep = x > 0
        shift = 1
    else:
        keep = x < nx - 1
        shift = lanes - 1

    def step(s, fresh):
        t = s if forward else steps - 1 - s
        from_x = jnp.where(keep, pltpu.roll(fresh, shift, 1), 0.0)
        right = rhs_ref[t]
        for j in range(count):
            right = right - kx_ref[t, j] * from_x[j : j + 1, :] - ky_ref[t, j] * fresh[j : j + 1, :]
        result = inv_ref[t, 0] * right[0:1, :]
        for j in range(1, count):
            result = result + inv_ref[t, j] * right[j : j + 1, :]
        out_ref[t] = result
        return result

    lax.fori_loop(0, steps, step, jnp.zeros((ROWS, lanes), jnp.float32), unroll=2)


def sweep(rhs, along_x, along_y, inverses, forward, nx):
    count = along_x.shape[1]
    kernel = functools.partial(sweep_kernel, forward=forward, nx=nx, count=count)
    return pl.pallas_call(
        kernel,
        out_shape=jax.ShapeDtypeStruct(rhs.shape, jnp.float32),
    )(rhs, along_x, along_y, inverses)


def per_device(
    adjoint_source,
    initial,
    inverses,
    couplings,
    interface_tiles,
    source_cells,
    target_cells,
    tile_counts,
):
    n_bx = lax.axis_size("bx")
    n_by = lax.axis_size("by")
    devices = n_bx * n_by
    count, ca, cb, nz = adjoint_source.shape
    nx, ny = n_bx * ca, n_by * cb
    width = nz // devices
    steps = nx + ny
    tables = (interface_tiles, source_cells, target_cells, tile_counts)

    def to_z(values):
        vcount = values.shape[0]
        received = lax.all_to_all(to_slices(values, devices), AXES, 0, 0, tiled=True)
        return skew(gather_grid(received, n_bx, n_by, ca, cb, width), steps, nx)

    def to_xy(skewed):
        grid = unskew(skewed[:, :count], ny, nx)
        received = lax.all_to_all(scatter_grid(grid, n_bx, n_by, ca, cb, width), AXES, 0, 0, tiled=True)
        return from_slices(received, ca, cb)

    base = adjoint_source - interface(initial, *tables)
    packed = jnp.concatenate(
        [
            jnp.swapaxes(inverses, 0, 1).reshape(count * count, ca, cb, nz),
            jnp.swapaxes(couplings, 1, 2).astype(jnp.float32).reshape(6 * count * count, ca, cb, nz),
            base,
            initial,
        ],
        axis=0,
    )
    rows = to_z(packed)
    span = count * count
    inv = as_matrices(rows[:, :span], count)
    ks = [as_matrices(rows[:, span * (k + 1) : span * (k + 2)], count) for k in range(6)]
    base_z = as_vectors(rows[:, 7 * span : 7 * span + count])
    iterate = as_vectors(rows[:, 7 * span + count : 7 * span + 2 * count])

    for number in range(ITERS):
        if number > 0:
            inter = interface(to_xy(iterate), *tables)
            base_z = as_vectors(to_z(adjoint_source - inter))
        lower_terms = (
            base_z
            - matvec(ks[1], shift_x(shift_t(iterate, 1), 1, nx))
            - matvec(ks[3], shift_t(iterate, 1))
            - matvec(ks[4], shift_z(iterate, -1, nx, devices, count))
            - matvec(ks[5], shift_z(iterate, 1, nx, devices, count))
        )
        half = sweep(lower_terms, ks[0], ks[2], inv, True, nx)
        upper_terms = (
            base_z
            - matvec(ks[0], shift_x(shift_t(half, -1), -1, nx))
            - matvec(ks[2], shift_t(half, -1))
            - matvec(ks[4], shift_z(half, -1, nx, devices, count))
            - matvec(ks[5], shift_z(half, 1, nx, devices, count))
        )
        iterate = sweep(upper_terms, ks[1], ks[3], inv, False, nx)
    return to_xy(iterate)


def solution(mesh):
    return jax.shard_map(
        per_device,
        mesh=mesh,
        in_specs=(
            P(None, "bx", "by", None),
            P(None, "bx", "by", None),
            P(None, None, "bx", "by", None),
            P(None, None, None, "bx", "by", None),
            P(AXES, None, None, None),
            P(AXES, None),
            P(AXES, None),
            P(AXES, None),
        ),
        out_specs=P(None, "bx", "by", None),
        check_vma=False,
    )
```

time: 1230 us -> 692 us (0.56)
  starting transfers between devices: 586 us -> 63.6 us
  waiting for transfers between devices: 525 us -> 153 us
  local copies, waits for them, and re-layouts: 64.9 us -> 283 us
  other arithmetic: 37.1 us -> 119 us
  Pallas kernels: 0 us -> 48 us
  blocking collectives: 0 us -> 13.9 us
    ppermute x192 -> x8, starting transfers between devices: 564 us -> 28.6 us  [the longest x4 18.9 us: shift_z(): lax.ppermute(values[:, :count, :nx], AXES, [(i + 1, i) for i in range(dev...]
    ppermute x192 -> x8, waiting for transfers between devices: 525 us -> 26.2 us  [the longest x4 19.8 us: shift_z(): lax.ppermute(values[:, :count, -nx:], AXES, [(i, i + 1) for i in range(de...]
    all_to_all x2 -> x5, waiting for transfers between devices: 0.01 us -> 127 us  [the longest x2 108 us: to_z(): lax.all_to_all(to_slices(values, devices), AXES, 0, 0, tiled=True)]
    reshape x0 -> x22, local copies, waits for them, and re-layouts: none -> 92.1 us  [the longest x4 32.1 us: gather_grid(): return shaped.reshape(n_by * cb, count, width * n_bx * ca)]
    select_n x0 -> x24, other arithmetic: none -> 66.2 us  [the longest x10 63.5 us: skew(): values = jnp.where(x & bit != 0, moved, values)]
    transpose x0 -> x8, local copies, waits for them, and re-layouts: none -> 64.8 us  [the longest x2 20.1 us: from_slices(): return jnp.transpose(shaped, (3, 1, 2, 0))]
    slice x19 -> x59, local copies, waits for them, and re-layouts: 14.5 us -> 69.6 us  [the longest x10 40.4 us: skew(): values[:-bit]]
    pallas_call x0 -> x4, Pallas kernels: none -> 48 us  [sweep(): pl.pallas_call(kernel, out_shape=jax.ShapeDtypeStruct(rhs.shape, jnp.floa...]
  transfers between devices with their start and end apart: 194 -> 13, of which waited for: 108 -> 9; matrix products, arithmetic and copies ran while one was open for 3% -> 17% of each run, Pallas kernels for 0% -> 0%
where the time goes in v1:
time: 692 us; the launch traced here: 682 us
  local copies, waits for them, and re-layouts  283 us (41%)
  waiting for transfers between devices  153 us (22%)
  other arithmetic  119 us (17%)
  starting transfers between devices  63.6 us (9%)
  Pallas kernels  48 us (7%)
  blocking collectives  13.9 us (2%)
    all_to_all x2, waiting for transfers between devices, to_z(): lax.all_to_all(to_slices(values, devices), AXES, 0, 0, tiled=True)  108 us
    select_n x10, other arithmetic, skew(): values = jnp.where(x & bit != 0, moved, values)  63.5 us
    pallas_call x4, Pallas kernels, sweep(): pl.pallas_call(kernel, out_shape=jax.ShapeDtypeStruct(rhs.shape, jnp.floa...  48 us
    slice x10, local copies, waits for them, and re-layouts, skew(): values[:-bit]  40.4 us
    reshape x4, local copies, waits for them, and re-layouts, gather_grid(): return shaped.reshape(n_by * cb, count, width * n_bx * ca)  32.1 us
    transpose x2, local copies, waits for them, and re-layouts, from_slices(): return jnp.transpose(shaped, (3, 1, 2, 0))  20.1 us
    ppermute x4, waiting for transfers between devices, shift_z(): lax.ppermute(values[:, :count, -nx:], AXES, [(i, i + 1) for i in range(de...  19.8 us
    ppermute x4, starting transfers between devices, shift_z(): lax.ppermute(values[:, :count, :nx], AXES, [(i + 1, i) for i in range(dev...  18.9 us
  transfers between devices with their start and end apart: 13, of which 9 were waited for; matrix products, arithmetic and copies ran while one was open for 17% of the time, Pallas kernels for 0%

profile of v1, /device:TPU:1, one launch (start us, length us, event | category | flops | bytes accessed | tf_op | source)
XLA Modules:
  0.0 681.7 jit_solution(12928289125160470950)
XLA Ops:
  1.4 3.7 copy.115
  5.7 2.9 gather_fusion
  10.5 11.5 %all-to-all-start = ((f32[5,128,2]{0,2,1:T(2,128)}), f32[5,128,2]{0,2,1:T(2,128)S(1)}, u32[]{:S(2)}, u32[]{:S(2)}) async-start(f32[5,128,2]{0,2,1:T(2,128)} %broadcast_select_fusion.1), calls=%async_computation | async-start | bytes 262144 | tf_op jit(solution)/shard_map/all_to_all | solution.py:26
  22.9 4.1 copy.114
  27.1 5.0 all-to-all-done
  32.0 3.6 scatter_custom_fusion
  35.7 2.9 copy.118
  38.7 11.6 %maximum_bitcast_fusion = f32[512,4,4,185]{0,2,1,3:T(4,128)} fusion(f32[5,4,4,512]{3,2,1,0:T(4,128)S(1)} %copy-done.31, f32[5,4,4,512]{3,2,1,0:T(4,128)S(1)} %sub.54, f32[150,4,4,512]{3,2,1,0:T(4,128)} %bitcast.101, f32[25,4,4,512]{3,2,1,0:T(4,128)S(1)} %bitcast.114), kind=kLoop, calls=%fused_computation.19 | loop fusion | flops 4546560 | bytes 12124160 | tf_op jit(solution)/shard_map/transpose | solution.py:33
  50.3 12.7 %copy.119 = f32[512,4,4,185]{3,2,1,0:T(4,128)} copy(f32[512,4,4,185]{0,2,1,3:T(4,128)} %maximum_bitcast_fusion) | data formatting | bytes 12124160 | tf_op jit(solution)/shard_map/transpose | solution.py:33
  63.0 10.0 %reshape.165 = f32[128,64,185]{2,1,0:T(8,128)} reshape(f32[512,4,4,185]{3,2,1,0:T(4,128)} %copy.119) | data formatting | bytes 12124160 | tf_op jit(solution)/shard_map/reshape | solution.py:34
  73.0 5.6 all-to-all-start.1
  78.8 99.5 %all-to-all-done.1 = f32[128,64,185]{2,1,0:T(8,128)} async-done(((f32[128,64,185]{2,1,0:T(8,128)}), f32[128,64,185]{2,1,0:T(8,128)}, u32[]{:S(2)}, u32[]{:S(2)}) %all-to-all-start.1) | async-done | bytes 6062112 | tf_op jit(solution)/shard_map/all_to_all | solution.py:185
  178.3 11.5 %copy.120 = f32[128,64,185]{2,0,1:T(8,128)} copy(f32[128,64,185]{2,1,0:T(8,128)} %all-to-all-done.1) | data formatting | bytes 12124160 | tf_op jit(solution)/shard_map/all_to_all | solution.py:185
  189.8 12.0 %copy.121 = f32[16,4,185,4,8,4]{2,5,4,3,1,0:T(4,128)} copy(f32[16,4,185,4,8,4]{2,0,4,1,5,3:T(8,128)} %bitcast.86) | data formatting | bytes 12124160 | tf_op jit(solution)/shard_map/transpose | solution.py:40
  201.8 10.0 %reshape.167 = f32[64,185,128]{1,2,0:T(8,128)} reshape(f32[16,4,185,4,8,4]{2,5,4,3,1,0:T(4,128)} %copy.121) | data formatting | bytes 12124160 | tf_op jit(solution)/shard_map/reshape | solution.py:41
  211.8 9.1 %copy.122 = f32[64,185,128]{2,1,0:T(8,128)} copy(f32[64,185,128]{1,2,0:T(8,128)} %reshape.167) | data formatting | bytes 12124160 | tf_op jit(solution)/shard_map/reshape | solution.py:41
  220.9 7.9 %pad.93 = f32[96,185,128]{2,1,0:T(8,128)} pad(f32[64,185,128]{2,1,0:T(8,128)} %copy.122, f32[]{:T(128)} %constant.107.clone.1), padding=0_32x0_0x0_0 | pad | bytes 15155204 | tf_op jit(solution)/shard_map/jit(_pad)/pad | solution.py:64
  228.8 8.4 %slice.304 = f32[95,185,128]{2,1,0:T(8,128)} slice(f32[96,185,128]{2,1,0:T(8,128)} %pad.93), slice={[0:95], [0:185], [0:128]} | slice | bytes 17996800 | tf_op jit(solution)/shard_map/slice | solution.py:69
  237.3 12.8 %pad_select_fusion.4 = f32[96,185,128]{2,1,0:T(8,128)} fusion(f32[96,185,128]{2,1,0:T(8,128)} %pad.93, f32[95,185,128]{2,1,0:T(8,128)} %slice.304, s32[128]{0:T(128)S(1)} %iota_and_fusion, s32[128]{0:T(128)S(1)} %broadcast_add_fusion, pred[128]{0:T(512)(128)(4,1)S(1)} %compare_and_fusion.1), kind=kLoop, calls=%fused_computation.18 | loop fusion | flops 9093120 | bytes 27185792 | tf_op jit(solution)/shard_map/jit(_where)/select_n | solution.py:70
  250.1 8.4 %slice.305 = f32[94,185,128]{2,1,0:T(8,128)} slice(f32[96,185,128]{2,1,0:T(8,128)} %pad_select_fusion.4), slice={[0:94], [0:185], [0:128]} | slice | bytes 17807360 | tf_op jit(solution)/shard_map/slice | solution.py:69
  258.5 12.8 %pad_select_fusion.3 = f32[96,185,128]{2,1,0:T(8,128)} fusion(f32[96,185,128]{2,1,0:T(8,128)} %pad_select_fusion.4, f32[94,185,128]{2,1,0:T(8,128)} %slice.305, s32[128]{0:T(128)S(1)} %iota_and_fusion, s32[128]{0:T(128)S(1)} %broadcast_add_fusion, pred[128]{0:T(512)(128)(4,1)S(1)} %compare_and_fusion.1), kind=kLoop, calls=%fused_computation.17 | loop fusion | flops 9093120 | bytes 27091072 | tf_op jit(solution)/shard_map/jit(_where)/select_n | solution.py:70
  271.3 8.2 %slice.306 = f32[92,185,128]{2,1,0:T(8,128)} slice(f32[96,185,128]{2,1,0:T(8,128)} %pad_select_fusion.3), slice={[0:92], [0:185], [0:128]} | slice | bytes 17428480 | tf_op jit(solution)/shard_map/slice | solution.py:69
  279.5 12.7 %pad_select_fusion.2 = f32[96,185,128]{2,1,0:T(8,128)} fusion(f32[96,185,128]{2,1,0:T(8,128)} %pad_select_fusion.3, f32[92,185,128]{2,1,0:T(8,128)} %slice.306, s32[128]{0:T(128)S(1)} %iota_and_fusion, s32[128]{0:T(128)S(1)} %broadcast_add_fusion, pred[128]{0:T(512)(128)(4,1)S(1)} %compare_and_fusion.1), kind=kLoop, calls=%fused_computation.16 | loop fusion | flops 9093120 | bytes 26901632 | tf_op jit(solution)/shard_map/jit(_where)/select_n | solution.py:70
  292.2 7.9 %slice.307 = f32[88,185,128]{2,1,0:T(8,128)} slice(f32[96,185,128]{2,1,0:T(8,128)} %pad_select_fusion.2), slice={[0:88], [0:185], [0:128]} | slice | bytes 16670720 | tf_op jit(solution)/shard_map/slice | solution.py:69
  300.1 12.5 %pad_select_fusion.1 = f32[96,185,128]{2,1,0:T(8,128)} fusion(f32[96,185,128]{2,1,0:T(8,128)} %pad_select_fusion.2, f32[88,185,128]{2,1,0:T(8,128)} %slice.307, s32[128]{0:T(128)S(1)} %iota_and_fusion, s32[128]{0:T(128)S(1)} %broadcast_add_fusion, pred[128]{0:T(512)(128)(4,1)S(1)} %compare_and_fusion.1), kind=kLoop, calls=%fused_computation.15 | loop fusion | flops 9093120 | bytes 26522752 | tf_op jit(solution)/shard_map/jit(_where)/select_n | solution.py:70
  312.7 7.3 %slice.308 = f32[80,185,128]{2,1,0:T(8,128)} slice(f32[96,185,128]{2,1,0:T(8,128)} %pad_select_fusion.1), slice={[0:80], [0:185], [0:128]} | slice | bytes 15155200 | tf_op jit(solution)/shard_map/slice | solution.py:69
  320.0 12.4 %pad_select_fusion = f32[96,185,128]{2,1,0:T(8,128)} fusion(f32[96,185,128]{2,1,0:T(8,128)} %pad_select_fusion.1, f32[80,185,128]{2,1,0:T(8,128)} %slice.308, s32[128]{0:T(128)S(1)} %iota_and_fusion, s32[128]{0:T(128)S(1)} %broadcast_add_fusion, pred[128]{0:T(512)(128)(4,1)S(1)} %compare_and_fusion.1), kind=kLoop, calls=%fused_computation.14 | loop fusion | flops 9093120 | bytes 25764992 | tf_op jit(solution)/shard_map/jit(_where)/select_n | solution.py:70
  332.4 7.9 %fusion.28 = (f32[96,25,128]{2,1,0:T(8,128)S(1)}, f32[96,25,128]{2,1,0:T(8,128)S(1)}, f32[96,25,128]{2,1,0:T(8,128)S(1)}, f32[96,25,128]{2,1,0:T(8,128)}, f32[96...) fusion(f32[96,185,128]{2,1,0:T(8,128)} %pad_select_fusion), kind=kLoop, calls=%fused_computation.139 | loop fusion | bytes 17203200 | tf_op jit(solution)/shard_map/slice | solution.py:205
  344.0 6.0 collective-permute-start.1
  371.0 12.0 %shard_map.82 = f32[96,8,128]{2,1,0:T(8,128)} custom-call(f32[96,8,128]{2,1,0:T(8,128)} %copy_subtract_fusion.6.rhs_ref, f32[96,5,8,128]{3,2,1,0:T(8,128)} %pad.95.kx_ref, f32[96,5,8,128]{3,2,1,0:T(8,128)} %pad.103.ky_ref, f32[96,5,8,128]{3,2,1,0:T(8,128)} %pad.104.inv_ref), custom_call_target="tpu_custom_call" | custom-call | tf_op jit(solution)/shard_map/pallas_call | solution.py:158
  385.9 7.0 %collective-permute-start.3 = (f32[96,5,32]{2,1,0:T(8,128)S(1)}, f32[96,5,32]{2,1,0:T(8,128)S(1)}, u32[]{:S(2)}, u32[]{:S(2)}) collective-permute-start(f32[96,5,32]{2,1,0:T(8,128)S(1)} %get-tuple-element.30), channel_id=1, source_target_pairs={{1,0},{2,1},{3,2},{4,3},{5,4},{6,5},{7,6},{8,7},{9,8},{10,9},{11,1... | collective-permute-start | bytes 184328 | tf_op jit(solution)/shard_map/ppermute | solution.py:121
  392.8 2.3 collective-permute-start.2
  397.9 11.2 %collective-permute-done.2 = f32[96,5,32]{2,1,0:T(8,128)S(1)} collective-permute-done((f32[96,5,32]{2,1,0:T(8,128)S(1)}, f32[96,5,32]{2,1,0:T(8,128)S(1)}, u32[]{:S(2)}, u32[]{:S(2)}) %collective-permute-start.2) | collective-permute-done | bytes 61472 | tf_op jit(solution)/shard_map/ppermute | solution.py:124
  410.8 12.0 %shard_map.83 = f32[96,8,128]{2,1,0:T(8,128)} custom-call(f32[96,8,128]{2,1,0:T(8,128)} %copy_subtract_fusion.4.rhs_ref, f32[96,5,8,128]{3,2,1,0:T(8,128)} %get-tuple-element.19.kx_ref, f32[96,5,8,128]{3,2,1,0:T(8,128)} %get-tuple-element.17.ky_ref, f32[96,5,8,128]{3,2,1,0:T(8,128)} %pad.104.inv_ref), custom_call_target="tpu_custom_call" | custom-call | tf_op jit(solution)/shard_map/pallas_call | solution.py:158
  422.8 2.2 fusion.36
  429.3 3.4 collective-permute-start.4
  435.0 7.0 %reshape.175 = f32[16,4,5,4,8,4]{5,4,3,1,0,2:T(8,128)} reshape(f32[64,5,128]{2,0,1:T(8,128)S(1)} %copy.143) | data formatting | bytes 327680 | tf_op jit(solution)/shard_map/reshape | solution.py:46
  442.0 7.9 %copy.144 = f32[8,16,4,4,4,5]{1,0,4,3,2,5:T(8,128)} copy(f32[8,16,4,4,4,5]{3,0,2,4,1,5:T(8,128)} %bitcast.97) | data formatting | bytes 327680 | tf_op jit(solution)/shard_map/transpose | solution.py:47
  454.6 8.5 %all-to-all-start.2 = ((f32[128,1,320]{2,1,0:T(1,128)}), f32[128,1,320]{2,1,0:T(1,128)S(1)}, u32[]{:S(2)}, u32[]{:S(2)}) async-start(f32[128,1,320]{2,1,0:T(1,128)} %reshape.233), calls=%async_computation.2 | async-start | bytes 393216 | tf_op jit(solution)/shard_map/all_to_all | solution.py:190
  463.1 2.8 multiply_reduce_fusion.3
  467.8 5.9 all-to-all-done.2
  479.0 7.7 %reshape.177 = f32[512,4,4,5]{2,1,0,3:T(4,128)} reshape(f32[128,64,5]{1,0,2:T(8,128)S(1)} %copy.146) | data formatting | bytes 327680 | tf_op jit(solution)/shard_map/reshape | solution.py:54
  486.7 15.4 %copy.147 = f32[5,4,4,512]{0,3,2,1:T(8,128)} copy(f32[5,4,4,512]{2,1,3,0:T(4,128)} %bitcast.98) | data formatting | bytes 327680 | tf_op jit(solution)/shard_map/transpose | solution.py:55
  502.0 3.7 gather_fusion.1
  511.0 5.1 all-to-all-start.3
  518.3 7.8 %all-to-all-done.3 = f32[5,128,2]{0,2,1:T(2,128)} async-done(((f32[5,128,2]{0,2,1:T(2,128)}), f32[5,128,2]{0,2,1:T(2,128)}, u32[]{:S(2)}, u32[]{:S(2)}) %all-to-all-start.3) | async-done | bytes 5152 | tf_op jit(solution)/shard_map/all_to_all | solution.py:26
  526.1 4.1 scatter_custom_fusion.1
  530.3 2.9 copy.150
  533.9 4.6 copy.151
  538.5 7.0 %reshape.180 = f32[128,64,5]{1,0,2:T(8,128)S(1)} reshape(f32[512,4,4,5]{2,1,0,3:T(4,128)} %copy.151) | data formatting | bytes 327680 | tf_op jit(solution)/shard_map/reshape | solution.py:34
  548.6 4.2 all-to-all-start.4
  555.0 8.3 %all-to-all-done.4 = f32[128,1,320]{2,1,0:T(1,128)S(1)} async-done(((f32[128,1,320]{2,1,0:T(1,128)}), f32[128,1,320]{2,1,0:T(1,128)S(1)}, u32[]{:S(2)}, u32[]{:S(2)}) %all-to-all-start.4) | async-done | bytes 163872 | tf_op jit(solution)/shard_map/all_to_all | solution.py:185
  569.7 7.4 %copy.169 = f32[16,4,5,4,8,4]{5,4,3,2,1,0:T(8,128)} copy(f32[16,4,5,4,8,4]{0,4,1,5,3,2:T(8,128)} %bitcast.104) | data formatting | bytes 327680 | tf_op jit(solution)/shard_map/reshape | solution.py:41
  577.1 5.6 reshape.227
  585.7 12.0 %shard_map.84 = f32[96,8,128]{2,1,0:T(8,128)} custom-call(f32[96,8,128]{2,1,0:T(8,128)} %copy_subtract_fusion.2.rhs_ref, f32[96,5,8,128]{3,2,1,0:T(8,128)} %pad.95.kx_ref, f32[96,5,8,128]{3,2,1,0:T(8,128)} %pad.103.ky_ref, f32[96,5,8,128]{3,2,1,0:T(8,128)} %pad.104.inv_ref), custom_call_target="tpu_custom_call" | custom-call | tf_op jit(solution)/shard_map/pallas_call | solution.py:158
  600.5 4.0 collective-permute-start.7
  607.5 4.9 collective-permute-done.7
  612.4 8.6 %collective-permute-done.6 = f32[96,5,32]{2,1,0:T(8,128)S(1)} collective-permute-done((f32[96,5,32]{2,1,0:T(8,128)S(1)}, f32[96,5,32]{2,1,0:T(8,128)S(1)}, u32[]{:S(2)}, u32[]{:S(2)}) %collective-permute-start.6) | collective-permute-done | bytes 61472 | tf_op jit(solution)/shard_map/ppermute | solution.py:124
  623.5 12.0 %shard_map.85 = f32[96,8,128]{2,1,0:T(8,128)} custom-call(f32[96,8,128]{2,1,0:T(8,128)} %copy_subtract_fusion.rhs_ref, f32[96,5,8,128]{3,2,1,0:T(8,128)} %get-tuple-element.19.kx_ref, f32[96,5,8,128]{3,2,1,0:T(8,128)} %get-tuple-element.17.ky_ref, f32[96,5,8,128]{3,2,1,0:T(8,128)} %pad.104.inv_ref), custom_call_target="tpu_custom_call" | custom-call | tf_op jit(solution)/shard_map/pallas_call | solution.py:158
  638.6 6.9 %reshape.183 = f32[16,4,5,4,8,4]{5,4,3,1,0,2:T(8,128)} reshape(f32[64,5,128]{2,0,1:T(8,128)S(1)} %copy.164) | data formatting | bytes 327680 | tf_op jit(solution)/shard_map/reshape | solution.py:46
  645.6 7.3 %copy.165 = f32[8,16,4,4,4,5]{1,0,4,3,2,5:T(8,128)S(1)} copy(f32[8,16,4,4,4,5]{3,0,2,4,1,5:T(8,128)} %bitcast.99) | data formatting | bytes 327680 | tf_op jit(solution)/shard_map/transpose | solution.py:47
  653.8 13.9 %all_to_all.38 = f32[128,1,320]{2,1,0:T(1,128)S(1)} all-to-all(f32[128,1,320]{2,1,0:T(1,128)S(1)} %reshape.237), channel_id=1, replica_groups=mesh['bx'=8,'by'=16] {'bx','by'}, dimensions={0} | all-to-all | bytes 327680 | tf_op jit(solution)/shard_map/all_to_all | solution.py:190
  669.0 7.7 %reshape.185 = f32[512,4,4,5]{2,1,0,3:T(4,128)} reshape(f32[128,64,5]{1,0,2:T(8,128)S(1)} %copy.167) | data formatting | bytes 327680 | tf_op jit(solution)/shard_map/reshape | solution.py:54
  676.7 4.8 copy.168
  (244 shorter events, 90.9 us)
Async XLA Ops:
  1.4 7.4 %copy-start.39 = (pred[256]{0:T(512)(128)(4,1)}, pred[256]{0:T(512)(128)(4,1)S(1)}, u32[]{:S(2)}) copy-start(pred[256]{0:T(512)(128)(4,1)S(1)} %compare_and_fusion) | copy-start | bytes 772
  1.4 7.4 %copy-start.36 = (f32[1,5,5,256]{3,0,2,1:T(1,128)S(1)}, f32[1,5,5,256]{3,0,2,1:T(1,128)}, u32[]{:S(2)}) copy-start(f32[1,5,5,256]{3,0,2,1:T(1,128)} %param.14) | copy-start | bytes 76804
  1.4 7.6 %copy-start.43 = (s32[1,128]{1,0:T(1,128)S(1)}, s32[1,128]{1,0:T(1,128)}, u32[]{:S(2)}) copy-start(s32[1,128]{1,0:T(1,128)} %param.17) | copy-start | bytes 1540
  1.4 20.6 %copy-start.19 = (bf16[6,5,5,4,4,512]{5,4,3,2,1,0:T(4,128)(2,1)S(1)}, bf16[6,5,5,4,4,512]{5,4,3,2,1,0:T(4,128)(2,1)}, u32[]{:S(2)}) copy-start(bf16[6,5,5,4,4,512]{5,4,3,2,1,0:T(4,128)(2,1)} %param.13) | copy-start | bytes 7372804
  5.1 0.6 copy-start.38
  9.0 0.6 copy-start.34
  10.5 21.5 %all-to-all-start = ((f32[5,128,2]{0,2,1:T(2,128)}), f32[5,128,2]{0,2,1:T(2,128)S(1)}, u32[]{:S(2)}, u32[]{:S(2)}) async-start(f32[5,128,2]{0,2,1:T(2,128)} %broadcast_select_fusion.1), calls=%async_computation | async-start | bytes 262144 | tf_op jit(solution)/shard_map/all_to_all | solution.py:26
  22.0 0.8 copy-start.41
  22.9 9.2 %copy-start.42 = (s32[256,1]{0,1:T(1,128)}, s32[256,1]{0,1:T(1,128)S(1)}, u32[]{:S(2)}) copy-start(s32[256,1]{0,1:T(1,128)S(1)} %compare_select_fusion) | copy-start | bytes 3076
  22.9 4.2 copy-start.28
  35.7 2.9 copy-start.29
  35.7 3.0 copy-start.31
  73.0 105.3 %all-to-all-start.1 = ((f32[128,64,185]{2,1,0:T(8,128)}), f32[128,64,185]{2,1,0:T(8,128)}, u32[]{:S(2)}, u32[]{:S(2)}) async-start(f32[128,64,185]{2,1,0:T(8,128)} %reshape.165), calls=%async_computation.1 | async-start | bytes 16777216 | tf_op jit(solution)/shard_map/all_to_all | solution.py:185
  78.7 356.2 %copy-start.32 = (pred[96,5,128]{2,1,0:T(8,128)(4,1)}, pred[96,5,128]{2,1,0:T(8,128)(4,1)S(1)}, u32[]{:S(2)}) copy-start(pred[96,5,128]{2,1,0:T(8,128)(4,1)S(1)} %fusion.17) | copy-start | bytes 184324
  78.8 316.7 %copy-start.26 = (pred[96,8,128]{2,1,0:T(8,128)(4,1)}, pred[96,8,128]{2,1,0:T(8,128)(4,1)S(1)}, u32[]{:S(2)}) copy-start(pred[96,8,128]{2,1,0:T(8,128)(4,1)S(1)} %get-tuple-element.35) | copy-start | bytes 294916
  341.8 28.0 %copy-start.17 = (f32[96,5,128]{2,1,0:T(8,128)}, f32[96,5,128]{2,1,0:T(8,128)S(1)}, u32[]{:S(2)}) copy-start(f32[96,5,128]{2,1,0:T(8,128)S(1)} %get-tuple-element.13) | copy-start | bytes 737284
  341.8 8.2 %copy-start.14 = (f32[96,25,128]{2,1,0:T(8,128)S(1)}, f32[96,25,128]{2,1,0:T(8,128)}, u32[]{:S(2)}) copy-start(f32[96,25,128]{2,1,0:T(8,128)} %get-tuple-element.9) | copy-start | bytes 3686404
  343.8 8.9 %copy-start.13 = (f32[96,25,128]{2,1,0:T(8,128)S(1)}, f32[96,25,128]{2,1,0:T(8,128)}, u32[]{:S(2)}) copy-start(f32[96,25,128]{2,1,0:T(8,128)} %get-tuple-element.10) | copy-start | bytes 3686404
  344.0 25.1 %collective-permute-start.1 = (f32[96,5,32]{2,1,0:T(8,128)S(1)}, f32[96,5,32]{2,1,0:T(8,128)S(1)}, u32[]{:S(2)}, u32[]{:S(2)}) collective-permute-start(f32[96,5,32]{2,1,0:T(8,128)S(1)} %get-tuple-element.16), channel_id=1, source_target_pairs={{1,0},{2,1},{3,2},{4,3},{5,4},{6,5},{7,6},{8,7},{9,8},{10,9},{11,1... | collective-permute-start | bytes 184328 | tf_op jit(solution)/shard_map/ppermute | solution.py:121
  350.7 18.5 %collective-permute-start = (f32[96,5,32]{2,1,0:T(8,128)S(1)}, f32[96,5,32]{2,1,0:T(8,128)S(1)}, u32[]{:S(2)}, u32[]{:S(2)}) collective-permute-start(f32[96,5,32]{2,1,0:T(8,128)S(1)} %get-tuple-element.15), channel_id=1, source_target_pairs={{0,1},{1,2},{2,3},{3,4},{4,5},{5,6},{6,7},{7,8},{8,9},{9,10},{10,1... | collective-permute-start | bytes 184328 | tf_op jit(solution)/shard_map/ppermute | solution.py:124
  352.7 1.5 copy-start.12
  354.2 1.5 copy-start.8
  355.7 2.0 copy-start.7
  360.1 9.5 %copy-start.3 = (f32[96,25,128]{2,0,1:T(8,128)}, f32[96,25,128]{2,0,1:T(8,128)S(1)}, u32[]{:S(2)}) copy-start(f32[96,25,128]{2,0,1:T(8,128)S(1)} %copy.132) | copy-start | bytes 3686404
  364.4 2.4 copy-start
  383.0 2.7 copy-start.11
  383.0 12.1 %copy-start.1 = (f32[96,5,5,128]{3,2,1,0:T(8,128)S(1)}, f32[96,5,5,128]{3,2,1,0:T(8,128)}, u32[]{:S(2)}) copy-start(f32[96,5,5,128]{3,2,1,0:T(8,128)} %copy-done) | copy-start | bytes 3686404
  385.9 11.7 %collective-permute-start.3 = (f32[96,5,32]{2,1,0:T(8,128)S(1)}, f32[96,5,32]{2,1,0:T(8,128)S(1)}, u32[]{:S(2)}, u32[]{:S(2)}) collective-permute-start(f32[96,5,32]{2,1,0:T(8,128)S(1)} %get-tuple-element.30), channel_id=1, source_target_pairs={{1,0},{2,1},{3,2},{4,3},{5,4},{6,5},{7,6},{8,7},{9,8},{10,9},{11,1... | collective-permute-start | bytes 184328 | tf_op jit(solution)/shard_map/ppermute | solution.py:121
  392.8 16.3 %collective-permute-start.2 = (f32[96,5,32]{2,1,0:T(8,128)S(1)}, f32[96,5,32]{2,1,0:T(8,128)S(1)}, u32[]{:S(2)}, u32[]{:S(2)}) collective-permute-start(f32[96,5,32]{2,1,0:T(8,128)S(1)} %get-tuple-element.29), channel_id=1, source_target_pairs={{0,1},{1,2},{2,3},{3,4},{4,5},{5,6},{6,7},{7,8},{8,9},{9,10},{10,1... | collective-permute-start | bytes 184328 | tf_op jit(solution)/shard_map/ppermute | solution.py:124
  395.6 2.1 copy-start.4
  397.8 11.7 %copy-start.18 = (f32[96,5,128]{2,1,0:T(8,128)S(1)}, f32[96,5,128]{2,1,0:T(8,128)}, u32[]{:S(2)}) copy-start(f32[96,5,128]{2,1,0:T(8,128)} %copy-done.17) | copy-start | bytes 737284
  422.8 4.4 copy-start.6
  422.8 9.9 %copy-start.9 = (f32[96,5,5,128]{3,2,1,0:T(8,128)S(1)}, f32[96,5,5,128]{3,2,1,0:T(8,128)}, u32[]{:S(2)}) copy-start(f32[96,5,5,128]{3,2,1,0:T(8,128)} %copy-done.8) | copy-start | bytes 3686404
  427.4 38.5 %collective-permute-start.5 = (f32[96,5,32]{2,1,0:T(8,128)}, f32[96,5,32]{2,1,0:T(8,128)}, u32[]{:S(2)}, u32[]{:S(2)}) collective-permute-start(f32[96,5,32]{2,1,0:T(8,128)} %get-tuple-element.26), channel_id=1, source_target_pairs={{1,0},{2,1},{3,2},{4,3},{5,4},{6,5},{7,6},{8,7},{9,8},{10,9},{11,1... | collective-permute-start | bytes 184328 | tf_op jit(solution)/shard_map/ppermute | solution.py:121
  429.3 123.5 %collective-permute-start.4 = (f32[96,5,32]{2,1,0:T(8,128)}, f32[96,5,32]{2,1,0:T(8,128)}, u32[]{:S(2)}, u32[]{:S(2)}) collective-permute-start(f32[96,5,32]{2,1,0:T(8,128)} %get-tuple-element.25), channel_id=1, source_target_pairs={{0,1},{1,2},{2,3},{3,4},{4,5},{5,6},{6,7},{7,8},{8,9},{9,10},{10,1... | collective-permute-start | bytes 184328 | tf_op jit(solution)/shard_map/ppermute | solution.py:124
  454.6 19.1 %all-to-all-start.2 = ((f32[128,1,320]{2,1,0:T(1,128)}), f32[128,1,320]{2,1,0:T(1,128)S(1)}, u32[]{:S(2)}, u32[]{:S(2)}) async-start(f32[128,1,320]{2,1,0:T(1,128)} %reshape.233), calls=%async_computation.2 | async-start | bytes 393216 | tf_op jit(solution)/shard_map/all_to_all | solution.py:190
  463.1 2.8 copy-start.24
  486.7 19.0 %copy-start.40 = (pred[256]{0:T(512)(128)(4,1)S(1)}, pred[256]{0:T(512)(128)(4,1)}, u32[]{:S(2)}) copy-start(pred[256]{0:T(512)(128)(4,1)} %copy-done.39) | copy-start | bytes 772
  486.7 21.7 %copy-start.37 = (f32[1,5,5,256]{3,0,2,1:T(1,128)S(1)}, f32[1,5,5,256]{3,0,2,1:T(1,128)}, u32[]{:S(2)}) copy-start(f32[1,5,5,256]{3,0,2,1:T(1,128)} %param.14) | copy-start | bytes 76804
  486.7 22.5 %copy-start.35 = (pred[128,2]{1,0:T(8,128)(4,1)S(1)}, pred[128,2]{1,0:T(8,128)(4,1)}, u32[]{:S(2)}) copy-start(pred[128,2]{1,0:T(8,128)(4,1)} %copy-done.34) | copy-start | bytes 772
  486.7 29.4 %copy-start.25 = (f32[96,5,128]{2,0,1:T(8,128)S(1)}, f32[96,5,128]{2,0,1:T(8,128)}, u32[]{:S(2)}) copy-start(f32[96,5,128]{2,0,1:T(8,128)} %copy.158) | copy-start | bytes 737284
  511.0 15.2 %all-to-all-start.3 = ((f32[5,128,2]{0,2,1:T(2,128)}), f32[5,128,2]{0,2,1:T(2,128)}, u32[]{:S(2)}, u32[]{:S(2)}) async-start(f32[5,128,2]{0,2,1:T(2,128)} %broadcast_select_fusion), calls=%async_computation.3 | async-start | bytes 262144 | tf_op jit(solution)/shard_map/all_to_all | solution.py:26
  530.2 2.9 copy-start.30
  548.6 14.8 %all-to-all-start.4 = ((f32[128,1,320]{2,1,0:T(1,128)}), f32[128,1,320]{2,1,0:T(1,128)S(1)}, u32[]{:S(2)}, u32[]{:S(2)}) async-start(f32[128,1,320]{2,1,0:T(1,128)} %reshape.235), calls=%async_computation.4 | async-start | bytes 393216 | tf_op jit(solution)/shard_map/all_to_all | solution.py:185
  582.9 1.0 copy-start.20
  582.9 1.1 copy-start.21
  582.9 1.4 copy-start.22
  582.9 1.5 copy-start.23
  583.2 0.7 copy-start.15
  597.7 2.8 copy-start.10
  597.7 9.0 %copy-start.27 = (pred[96,8,128]{2,1,0:T(8,128)(4,1)S(1)}, pred[96,8,128]{2,1,0:T(8,128)(4,1)}, u32[]{:S(2)}) copy-start(pred[96,8,128]{2,1,0:T(8,128)(4,1)} %copy-done.26) | copy-start | bytes 294916
  599.0 7.8 %copy-start.2 = (f32[96,5,5,128]{3,2,1,0:T(8,128)S(1)}, f32[96,5,5,128]{3,2,1,0:T(8,128)}, u32[]{:S(2)}) copy-start(f32[96,5,5,128]{3,2,1,0:T(8,128)} %copy-done) | copy-start | bytes 3686404
  600.5 11.9 %collective-permute-start.7 = (f32[96,5,32]{2,1,0:T(8,128)S(1)}, f32[96,5,32]{2,1,0:T(8,128)S(1)}, u32[]{:S(2)}, u32[]{:S(2)}) collective-permute-start(f32[96,5,32]{2,1,0:T(8,128)S(1)} %get-tuple-element.22), channel_id=1, source_target_pairs={{1,0},{2,1},{3,2},{4,3},{5,4},{6,5},{7,6},{8,7},{9,8},{10,9},{11,1... | collective-permute-start | bytes 184328 | tf_op jit(solution)/shard_map/ppermute | solution.py:121
  604.5 16.5 %collective-permute-start.6 = (f32[96,5,32]{2,1,0:T(8,128)S(1)}, f32[96,5,32]{2,1,0:T(8,128)S(1)}, u32[]{:S(2)}, u32[]{:S(2)}) collective-permute-start(f32[96,5,32]{2,1,0:T(8,128)S(1)} %get-tuple-element.21), channel_id=1, source_target_pairs={{0,1},{1,2},{2,3},{3,4},{4,5},{5,6},{6,7},{7,8},{8,9},{9,10},{10,1... | collective-permute-start | bytes 184328 | tf_op jit(solution)/shard_map/ppermute | solution.py:124
  607.5 13.9 %copy-start.5 = (f32[96,25,128]{2,0,1:T(8,128)S(1)}, f32[96,25,128]{2,0,1:T(8,128)}, u32[]{:S(2)}) copy-start(f32[96,25,128]{2,0,1:T(8,128)} %copy-done.3) | copy-start | bytes 3686404
  621.3 1.0 copy-start.16
  637.7 0.9 copy-start.33

commit v2 on v1

--- a/solution.py
+++ b/solution.py
@@ -70,6 +70,35 @@
         values = jnp.where((x & bit) != 0, moved, values)
         bit *= 2
     return values
+
+
+def skew_kernel(grid_ref, out_ref, *, nx):
+    ny = grid_ref.shape[0]
+    steps = out_ref.shape[0]
+    out_ref[:ny] = grid_ref[...]
+    out_ref[ny:] = jnp.zeros((steps - ny,) + out_ref.shape[1:], jnp.float32)
+    x = lax.broadcasted_iota(jnp.int32, out_ref.shape[1:], 1) % nx
+    bit = 1
+    while bit < nx:
+        moves = (x & bit) != 0
+
+        def body(i, carry, bit=bit, moves=moves):
+            t = steps - 1 - i
+            out_ref[t] = jnp.where(moves, out_ref[t - bit], out_ref[t])
+            return carry
+
+        lax.fori_loop(0, steps - bit, body, 0)
+        for t in range(bit):
+            out_ref[t] = jnp.where(moves, 0.0, out_ref[t])
+        bit *= 2
+
+
+def skew_big(grid, steps, nx):
+    ny, count, lanes = grid.shape
+    return pl.pallas_call(
+        functools.partial(skew_kernel, nx=nx),
+        out_shape=jax.ShapeDtypeStruct((steps, count, lanes), jnp.float32),
+    )(grid)
 
 
 def unskew(values, ny, nx):
@@ -180,10 +209,9 @@
     steps = nx + ny
     tables = (interface_tiles, source_cells, target_cells, tile_counts)
 
-    def to_z(values):
-        vcount = values.shape[0]
+    def to_z(values, skewer=skew):
         received = lax.all_to_all(to_slices(values, devices), AXES, 0, 0, tiled=True)
-        return skew(gather_grid(received, n_bx, n_by, ca, cb, width), steps, nx)
+        return skewer(gather_grid(received, n_bx, n_by, ca, cb, width), steps, nx)
 
     def to_xy(skewed):
         grid = unskew(skewed[:, :count], ny, nx)
@@ -200,7 +228,7 @@
         ],
         axis=0,
     )
-    rows = to_z(packed)
+    rows = to_z(packed, skew_big)
     span = count * count
     inv = as_matrices(rows[:, :span], count)
     ks = [as_matrices(rows[:, span * (k + 1) : span * (k + 2)], count) for k in range(6)]

time: 692 us -> 600 us (0.87)
  other arithmetic: 119 us -> 55.9 us
  local copies, waits for them, and re-layouts: 283 us -> 239 us
  waiting for transfers between devices: 153 us -> 134 us
  starting transfers between devices: 63.6 us -> 82.1 us
  Pallas kernels: 48 us -> 62.2 us
    select_n x10 -> x5, other arithmetic: 63.5 us -> 0.25 us  [skew(): values = jnp.where(x & bit != 0, moved, values)]
    slice x10 -> x5, local copies, waits for them, and re-layouts: 40.4 us -> 0.13 us  [skew(): values[:-bit]]
    ppermute x4, starting transfers between devices: 18.9 us -> 36.2 us  [shift_z(): lax.ppermute(values[:, :count, :nx], AXES, [(i + 1, i) for i in range(dev...]
    pallas_call x0 -> x1, Pallas kernels: none -> 13.8 us  [skew_big(): pl.pallas_call(functools.partial(skew_kernel, nx=nx), out_shape=jax.Shape...]
    pad x2 -> x1, local copies, waits for them, and re-layouts: 7.95 us -> 0.03 us  [skew(): values = jnp.pad(grid, ((0, steps - ny), (0, 0), (0, 0)))]
    unnamed x95 -> x93, local copies, waits for them, and re-layouts: 15.5 us -> 19.4 us
  transfers between devices with their start and end apart: 13 -> 13, of which waited for: 9 -> 6; matrix products, arithmetic and copies ran while one was open for 17% -> 19% of each run, Pallas kernels for 0% -> 0%
where the time goes in v2:
time: 600 us; the launch traced here: 594 us
  local copies, waits for them, and re-layouts  239 us (40%)
  waiting for transfers between devices  134 us (22%)
  starting transfers between devices  82.1 us (14%)
  Pallas kernels  62.2 us (10%)
  other arithmetic  55.9 us (9%)
  blocking collectives  19.5 us (3%)
    all_to_all x2, waiting for transfers between devices, to_z(): lax.all_to_all(to_slices(values, devices), AXES, 0, 0, tiled=True)  106 us
    pallas_call x4, Pallas kernels, sweep(): pl.pallas_call(kernel, out_shape=jax.ShapeDtypeStruct(rhs.shape, jnp.floa...  48.4 us
    ppermute x4, starting transfers between devices, shift_z(): lax.ppermute(values[:, :count, :nx], AXES, [(i + 1, i) for i in range(dev...  36.2 us
    reshape x4, local copies, waits for them, and re-layouts, gather_grid(): return shaped.reshape(n_by * cb, count, width * n_bx * ca)  31.7 us
    transpose x2, local copies, waits for them, and re-layouts, from_slices(): return jnp.transpose(shaped, (3, 1, 2, 0))  20.1 us
    all_to_all x1, blocking collectives, to_xy(): lax.all_to_all(scatter_grid(grid, n_bx, n_by, ca, cb, width), AXES, 0, 0,...  19.5 us
    unnamed x93, local copies, waits for them, and re-layouts  19.4 us
    reshape x3, local copies, waits for them, and re-layouts, to_slices(): return shaped.reshape(devices, nz // devices * ca * cb, count)  18 us
  transfers between devices with their start and end apart: 13, of which 6 were waited for; matrix products, arithmetic and copies ran while one was open for 19% of the time, Pallas kernels for 0%

profile of v2, /device:TPU:1, one launch (start us, length us, event | category | flops | bytes accessed | tf_op | source)
XLA Modules:
  0.0 594.0 jit_solution(11480634886818625580)
XLA Ops:
  2.1 3.7 copy.115
  5.8 2.9 gather_fusion
  10.0 11.5 %all-to-all-start = ((f32[5,128,2]{0,2,1:T(2,128)}), f32[5,128,2]{0,2,1:T(2,128)S(1)}, u32[]{:S(2)}, u32[]{:S(2)}) async-start(f32[5,128,2]{0,2,1:T(2,128)} %broadcast_select_fusion.1), calls=%async_computation | async-start | bytes 262144 | tf_op jit(solution)/shard_map/all_to_all | solution.py:26
  22.7 4.1 copy.114
  26.8 4.7 all-to-all-done
  31.5 3.7 scatter_custom_fusion
  35.2 2.9 copy.118
  38.2 11.6 %maximum_bitcast_fusion = f32[512,4,4,185]{0,2,1,3:T(4,128)} fusion(f32[5,4,4,512]{3,2,1,0:T(4,128)S(1)} %copy-done.34, f32[5,4,4,512]{3,2,1,0:T(4,128)S(1)} %sub.54, f32[150,4,4,512]{3,2,1,0:T(4,128)} %bitcast.101, f32[25,4,4,512]{3,2,1,0:T(4,128)S(1)} %bitcast.114), kind=kLoop, calls=%fused_computation.4 | loop fusion | flops 4546560 | bytes 12124160 | tf_op jit(solution)/shard_map/transpose | solution.py:33
  49.8 12.7 %copy.119 = f32[512,4,4,185]{3,2,1,0:T(4,128)} copy(f32[512,4,4,185]{0,2,1,3:T(4,128)} %maximum_bitcast_fusion) | data formatting | bytes 12124160 | tf_op jit(solution)/shard_map/transpose | solution.py:33
  62.5 10.0 %reshape.165 = f32[128,64,185]{2,1,0:T(8,128)} reshape(f32[512,4,4,185]{3,2,1,0:T(4,128)} %copy.119) | data formatting | bytes 12124160 | tf_op jit(solution)/shard_map/reshape | solution.py:34
  72.5 6.0 %all-to-all-start.1 = ((f32[128,64,185]{2,1,0:T(8,128)}), f32[128,64,185]{2,1,0:T(8,128)}, u32[]{:S(2)}, u32[]{:S(2)}) async-start(f32[128,64,185]{2,1,0:T(8,128)} %reshape.165), calls=%async_computation.1 | async-start | bytes 16777216 | tf_op jit(solution)/shard_map/all_to_all | solution.py:213
  79.9 98.1 %all-to-all-done.1 = f32[128,64,185]{2,1,0:T(8,128)} async-done(((f32[128,64,185]{2,1,0:T(8,128)}), f32[128,64,185]{2,1,0:T(8,128)}, u32[]{:S(2)}, u32[]{:S(2)}) %all-to-all-start.1) | async-done | bytes 6062112 | tf_op jit(solution)/shard_map/all_to_all | solution.py:213
  178.1 11.5 %copy.120 = f32[128,64,185]{2,0,1:T(8,128)} copy(f32[128,64,185]{2,1,0:T(8,128)} %all-to-all-done.1) | data formatting | bytes 12124160 | tf_op jit(solution)/shard_map/all_to_all | solution.py:213
  189.5 12.0 %copy.121 = f32[16,4,185,4,8,4]{2,5,4,3,1,0:T(4,128)} copy(f32[16,4,185,4,8,4]{2,0,4,1,5,3:T(8,128)} %bitcast.86) | data formatting | bytes 12124160 | tf_op jit(solution)/shard_map/transpose | solution.py:40
  201.5 10.0 %reshape.167 = f32[64,185,128]{1,2,0:T(8,128)} reshape(f32[16,4,185,4,8,4]{2,5,4,3,1,0:T(4,128)} %copy.121) | data formatting | bytes 12124160 | tf_op jit(solution)/shard_map/reshape | solution.py:41
  211.5 8.7 %copy.122.grid_ref = f32[64,185,128]{2,1,0:T(8,128)} copy(f32[64,185,128]{1,2,0:T(8,128)} %reshape.167) | data formatting | bytes 12124160 | tf_op jit(solution)/shard_map/reshape | solution.py:41
  220.2 13.8 %shard_map.82 = f32[96,185,128]{2,1,0:T(8,128)} custom-call(f32[64,185,128]{2,1,0:T(8,128)} %copy.122.grid_ref), custom_call_target="tpu_custom_call" | custom-call | tf_op jit(solution)/shard_map/pallas_call | solution.py:98
  234.1 2.6 fusion.25
  236.6 2.2 fusion.24
  240.7 8.1 %fusion.23 = (f32[96,25,128]{2,1,0:T(8,128)S(1)}, f32[96,25,128]{2,1,0:T(8,128)S(1)}, f32[96,25,128]{2,1,0:T(8,128)S(1)}, f32[96,25,128]{2,1,0:T(8,128)S(1)}, f3...) fusion(f32[96,185,128]{2,1,0:T(8,128)} %shard_map.82), kind=kLoop, calls=%fused_computation.124 | loop fusion | bytes 17203200 | tf_op jit(solution)/shard_map/slice | solution.py:233
  248.8 1.9 collective-permute-start
  250.7 15.7 %collective-permute-start.1 = (f32[96,5,32]{2,1,0:T(8,128)}, f32[96,5,32]{2,1,0:T(8,128)S(1)}, u32[]{:S(2)}, u32[]{:S(2)}) collective-permute-start(f32[96,5,32]{2,1,0:T(8,128)} %get-tuple-element.16), channel_id=1, source_target_pairs={{1,0},{2,1},{3,2},{4,3},{5,4},{6,5},{7,6},{8,7},{9,8},{10,9},{11,1... | collective-permute-start | bytes 184328 | tf_op jit(solution)/shard_map/ppermute | solution.py:150
  266.4 2.1 copy.127
  273.3 1.8 fusion.26
  288.6 12.2 %shard_map.83 = f32[96,8,128]{2,1,0:T(8,128)} custom-call(f32[96,8,128]{2,1,0:T(8,128)} %copy_subtract_fusion.6.rhs_ref, f32[96,5,8,128]{3,2,1,0:T(8,128)} %pad.85.kx_ref, f32[96,5,8,128]{3,2,1,0:T(8,128)} %pad.93.ky_ref, f32[96,5,8,128]{3,2,1,0:T(8,128)} %pad.94.inv_ref), custom_call_target="tpu_custom_call" | custom-call | tf_op jit(solution)/shard_map/pallas_call | solution.py:187
  302.7 2.1 collective-permute-start.2
  305.2 7.0 %collective-permute-start.3 = (f32[96,5,32]{2,1,0:T(8,128)S(1)}, f32[96,5,32]{2,1,0:T(8,128)S(1)}, u32[]{:S(2)}, u32[]{:S(2)}) collective-permute-start(f32[96,5,32]{2,1,0:T(8,128)S(1)} %get-tuple-element.30), channel_id=1, source_target_pairs={{1,0},{2,1},{3,2},{4,3},{5,4},{6,5},{7,6},{8,7},{9,8},{10,9},{11,1... | collective-permute-start | bytes 184328 | tf_op jit(solution)/shard_map/ppermute | solution.py:150
  312.2 6.9 %collective-permute-done.2 = f32[96,5,32]{2,1,0:T(8,128)S(1)} collective-permute-done((f32[96,5,32]{2,1,0:T(8,128)S(1)}, f32[96,5,32]{2,1,0:T(8,128)S(1)}, u32[]{:S(2)}, u32[]{:S(2)}) %collective-permute-start.2) | collective-permute-done | bytes 61472 | tf_op jit(solution)/shard_map/ppermute | solution.py:153
  322.0 12.0 %shard_map.84 = f32[96,8,128]{2,1,0:T(8,128)} custom-call(f32[96,8,128]{2,1,0:T(8,128)} %copy_subtract_fusion.4.rhs_ref, f32[96,5,8,128]{3,2,1,0:T(8,128)} %get-tuple-element.19.kx_ref, f32[96,5,8,128]{3,2,1,0:T(8,128)} %get-tuple-element.17.ky_ref, f32[96,5,8,128]{3,2,1,0:T(8,128)} %pad.94.inv_ref), custom_call_target="tpu_custom_call" | custom-call | tf_op jit(solution)/shard_map/pallas_call | solution.py:187
  341.0 1.9 collective-permute-start.4
  342.9 6.9 %reshape.175 = f32[16,4,5,4,8,4]{5,4,3,1,0,2:T(8,128)} reshape(f32[64,5,128]{2,0,1:T(8,128)S(1)} %copy.143) | data formatting | bytes 327680 | tf_op jit(solution)/shard_map/reshape | solution.py:46
  349.9 7.9 %copy.144 = f32[8,16,4,4,4,5]{1,0,4,3,2,5:T(8,128)} copy(f32[8,16,4,4,4,5]{3,0,2,4,1,5:T(8,128)} %bitcast.97) | data formatting | bytes 327680 | tf_op jit(solution)/shard_map/transpose | solution.py:47
  360.4 2.0 reshape.233
  362.4 10.0 %all-to-all-start.2 = ((f32[128,1,320]{2,1,0:T(1,128)}), f32[128,1,320]{2,1,0:T(1,128)S(1)}, u32[]{:S(2)}, u32[]{:S(2)}) async-start(f32[128,1,320]{2,1,0:T(1,128)} %reshape.233), calls=%async_computation.2 | async-start | bytes 393216 | tf_op jit(solution)/shard_map/all_to_all | solution.py:218
  372.5 2.8 multiply_reduce_fusion.3
  375.2 7.0 %collective-permute-start.5 = (f32[96,5,32]{2,1,0:T(8,128)}, f32[96,5,32]{2,1,0:T(8,128)}, u32[]{:S(2)}, u32[]{:S(2)}) collective-permute-start(f32[96,5,32]{2,1,0:T(8,128)} %get-tuple-element.26), channel_id=1, source_target_pairs={{1,0},{2,1},{3,2},{4,3},{5,4},{6,5},{7,6},{8,7},{9,8},{10,9},{11,1... | collective-permute-start | bytes 184328 | tf_op jit(solution)/shard_map/ppermute | solution.py:150
  384.7 1.8 reduce
  386.5 1.8 reshape.234
  389.5 8.1 %reshape.177 = f32[512,4,4,5]{2,1,0,3:T(4,128)} reshape(f32[128,64,5]{1,0,2:T(8,128)S(1)} %copy.146) | data formatting | bytes 327680 | tf_op jit(solution)/shard_map/reshape | solution.py:54
  397.6 15.4 %copy.147 = f32[5,4,4,512]{0,3,2,1:T(8,128)} copy(f32[5,4,4,512]{2,1,3,0:T(4,128)} %bitcast.98) | data formatting | bytes 327680 | tf_op jit(solution)/shard_map/transpose | solution.py:55
  412.9 3.5 gather_fusion.1
  421.7 5.7 all-to-all-start.3
  428.3 9.0 %all-to-all-done.3 = f32[5,128,2]{0,2,1:T(2,128)} async-done(((f32[5,128,2]{0,2,1:T(2,128)}), f32[5,128,2]{0,2,1:T(2,128)}, u32[]{:S(2)}, u32[]{:S(2)}) %all-to-all-start.3) | async-done | bytes 5152 | tf_op jit(solution)/shard_map/all_to_all | solution.py:26
  437.3 3.9 scatter_custom_fusion.1
  441.3 2.9 copy.150
  444.9 4.5 copy.151
  449.5 7.0 %reshape.180 = f32[128,64,5]{1,0,2:T(8,128)S(1)} reshape(f32[512,4,4,5]{2,1,0,3:T(4,128)} %copy.151) | data formatting | bytes 327680 | tf_op jit(solution)/shard_map/reshape | solution.py:34
  457.5 2.0 reshape.235
  459.5 4.5 all-to-all-start.4
  466.4 8.1 %all-to-all-done.4 = f32[128,1,320]{2,1,0:T(1,128)S(1)} async-done(((f32[128,1,320]{2,1,0:T(1,128)}), f32[128,1,320]{2,1,0:T(1,128)S(1)}, u32[]{:S(2)}, u32[]{:S(2)}) %all-to-all-start.4) | async-done | bytes 163872 | tf_op jit(solution)/shard_map/all_to_all | solution.py:213
  474.5 1.8 reduce.1
  476.3 1.8 reshape.236
  480.8 7.4 %copy.169 = f32[16,4,5,4,8,4]{5,4,3,2,1,0:T(8,128)} copy(f32[16,4,5,4,8,4]{0,4,1,5,3,2:T(8,128)} %bitcast.104) | data formatting | bytes 327680 | tf_op jit(solution)/shard_map/reshape | solution.py:41
  488.2 5.6 reshape.227
  496.8 12.0 %shard_map.85 = f32[96,8,128]{2,1,0:T(8,128)} custom-call(f32[96,8,128]{2,1,0:T(8,128)} %copy_subtract_fusion.2.rhs_ref, f32[96,5,8,128]{3,2,1,0:T(8,128)} %pad.85.kx_ref, f32[96,5,8,128]{3,2,1,0:T(8,128)} %pad.93.ky_ref, f32[96,5,8,128]{3,2,1,0:T(8,128)} %pad.94.inv_ref), custom_call_target="tpu_custom_call" | custom-call | tf_op jit(solution)/shard_map/pallas_call | solution.py:187
  511.0 2.3 collective-permute-start.6
  513.3 6.6 %collective-permute-start.7 = (f32[96,5,32]{2,1,0:T(8,128)S(1)}, f32[96,5,32]{2,1,0:T(8,128)S(1)}, u32[]{:S(2)}, u32[]{:S(2)}) collective-permute-start(f32[96,5,32]{2,1,0:T(8,128)S(1)} %get-tuple-element.22), channel_id=1, source_target_pairs={{1,0},{2,1},{3,2},{4,3},{5,4},{6,5},{7,6},{8,7},{9,8},{10,9},{11,1... | collective-permute-start | bytes 184328 | tf_op jit(solution)/shard_map/ppermute | solution.py:150
  520.6 6.8 %collective-permute-done.6 = f32[96,5,32]{2,1,0:T(8,128)S(1)} collective-permute-done((f32[96,5,32]{2,1,0:T(8,128)S(1)}, f32[96,5,32]{2,1,0:T(8,128)S(1)}, u32[]{:S(2)}, u32[]{:S(2)}) %collective-permute-start.6) | collective-permute-done | bytes 61472 | tf_op jit(solution)/shard_map/ppermute | solution.py:153
  529.9 12.2 %shard_map.86 = f32[96,8,128]{2,1,0:T(8,128)} custom-call(f32[96,8,128]{2,1,0:T(8,128)} %copy_subtract_fusion.rhs_ref, f32[96,5,8,128]{3,2,1,0:T(8,128)} %get-tuple-element.19.kx_ref, f32[96,5,8,128]{3,2,1,0:T(8,128)} %get-tuple-element.17.ky_ref, f32[96,5,8,128]{3,2,1,0:T(8,128)} %pad.94.inv_ref), custom_call_target="tpu_custom_call" | custom-call | tf_op jit(solution)/shard_map/pallas_call | solution.py:187
  545.3 6.9 %reshape.183 = f32[16,4,5,4,8,4]{5,4,3,1,0,2:T(8,128)} reshape(f32[64,5,128]{2,0,1:T(8,128)S(1)} %copy.164) | data formatting | bytes 327680 | tf_op jit(solution)/shard_map/reshape | solution.py:46
  552.2 7.3 %copy.165 = f32[8,16,4,4,4,5]{1,0,4,3,2,5:T(8,128)S(1)} copy(f32[8,16,4,4,4,5]{3,0,2,4,1,5:T(8,128)} %bitcast.99) | data formatting | bytes 327680 | tf_op jit(solution)/shard_map/transpose | solution.py:47
  560.5 19.5 %all_to_all.38 = f32[128,1,320]{2,1,0:T(1,128)S(1)} all-to-all(f32[128,1,320]{2,1,0:T(1,128)S(1)} %reshape.237), channel_id=1, replica_groups=mesh['bx'=8,'by'=16] {'bx','by'}, dimensions={0} | all-to-all | bytes 327680 | tf_op jit(solution)/shard_map/all_to_all | solution.py:218
  581.3 7.7 %reshape.185 = f32[512,4,4,5]{2,1,0,3:T(4,128)} reshape(f32[128,64,5]{1,0,2:T(8,128)S(1)} %copy.167) | data formatting | bytes 327680 | tf_op jit(solution)/shard_map/reshape | solution.py:54
  589.0 4.8 copy.168
  (232 shorter events, 70.6 us)
Async XLA Ops:
  0.7 8.1 %copy-start.39 = (pred[256]{0:T(512)(128)(4,1)}, pred[256]{0:T(512)(128)(4,1)S(1)}, u32[]{:S(2)}) copy-start(pred[256]{0:T(512)(128)(4,1)S(1)} %compare_and_fusion) | copy-start | bytes 772
  2.1 6.8 %copy-start.37 = (f32[1,5,5,256]{3,0,2,1:T(1,128)S(1)}, f32[1,5,5,256]{3,0,2,1:T(1,128)}, u32[]{:S(2)}) copy-start(f32[1,5,5,256]{3,0,2,1:T(1,128)} %param.14) | copy-start | bytes 76804
  2.1 19.3 %copy-start.18 = (bf16[6,5,5,4,4,512]{5,4,3,2,1,0:T(4,128)(2,1)S(1)}, bf16[6,5,5,4,4,512]{5,4,3,2,1,0:T(4,128)(2,1)}, u32[]{:S(2)}) copy-start(bf16[6,5,5,4,4,512]{5,4,3,2,1,0:T(4,128)(2,1)} %param.13) | copy-start | bytes 7372804
  10.0 21.5 %all-to-all-start = ((f32[5,128,2]{0,2,1:T(2,128)}), f32[5,128,2]{0,2,1:T(2,128)S(1)}, u32[]{:S(2)}, u32[]{:S(2)}) async-start(f32[5,128,2]{0,2,1:T(2,128)} %broadcast_select_fusion.1), calls=%async_computation | async-start | bytes 262144 | tf_op jit(solution)/shard_map/all_to_all | solution.py:26
  21.5 0.9 copy-start.41
  21.5 1.2 copy-start.31
  22.4 9.2 %copy-start.42 = (s32[256,1]{0,1:T(1,128)}, s32[256,1]{0,1:T(1,128)S(1)}, u32[]{:S(2)}) copy-start(s32[256,1]{0,1:T(1,128)S(1)} %compare_select_fusion) | copy-start | bytes 3076
  35.2 2.9 copy-start.32
  35.2 3.0 copy-start.34
  72.5 105.6 %all-to-all-start.1 = ((f32[128,64,185]{2,1,0:T(8,128)}), f32[128,64,185]{2,1,0:T(8,128)}, u32[]{:S(2)}, u32[]{:S(2)}) async-start(f32[128,64,185]{2,1,0:T(8,128)} %reshape.165), calls=%async_computation.1 | async-start | bytes 16777216 | tf_op jit(solution)/shard_map/all_to_all | solution.py:213
  248.8 37.1 %collective-permute-start = (f32[96,5,32]{2,1,0:T(8,128)}, f32[96,5,32]{2,1,0:T(8,128)S(1)}, u32[]{:S(2)}, u32[]{:S(2)}) collective-permute-start(f32[96,5,32]{2,1,0:T(8,128)} %get-tuple-element.15), channel_id=1, source_target_pairs={{0,1},{1,2},{2,3},{3,4},{4,5},{5,6},{6,7},{7,8},{8,9},{9,10},{10,1... | collective-permute-start | bytes 184328 | tf_op jit(solution)/shard_map/ppermute | solution.py:153
  250.7 35.4 %collective-permute-start.1 = (f32[96,5,32]{2,1,0:T(8,128)}, f32[96,5,32]{2,1,0:T(8,128)S(1)}, u32[]{:S(2)}, u32[]{:S(2)}) collective-permute-start(f32[96,5,32]{2,1,0:T(8,128)} %get-tuple-element.16), channel_id=1, source_target_pairs={{1,0},{2,1},{3,2},{4,3},{5,4},{6,5},{7,6},{8,7},{9,8},{10,9},{11,1... | collective-permute-start | bytes 184328 | tf_op jit(solution)/shard_map/ppermute | solution.py:150
  268.5 1.4 copy-start.13
  269.3 4.1 copy-start.9
  270.6 1.0 copy-start.22
  270.6 1.0 copy-start.29
  271.4 1.9 copy-start.8
  271.7 1.7 copy-start.21
  280.4 6.0 %copy-start.3 = (f32[96,25,128]{2,0,1:T(8,128)}, f32[96,25,128]{2,0,1:T(8,128)S(1)}, u32[]{:S(2)}) copy-start(f32[96,25,128]{2,0,1:T(8,128)S(1)} %copy.132) | copy-start | bytes 3686404
  282.6 1.9 copy-start
  286.4 1.0 copy-start.16
  300.8 1.2 copy-start.12
  302.2 2.6 copy-start.27
  302.3 2.6 copy-start.1
  302.7 16.4 %collective-permute-start.2 = (f32[96,5,32]{2,1,0:T(8,128)S(1)}, f32[96,5,32]{2,1,0:T(8,128)S(1)}, u32[]{:S(2)}, u32[]{:S(2)}) collective-permute-start(f32[96,5,32]{2,1,0:T(8,128)S(1)} %get-tuple-element.29), channel_id=1, source_target_pairs={{0,1},{1,2},{2,3},{3,4},{4,5},{5,6},{6,7},{7,8},{8,9},{9,10},{10,1... | collective-permute-start | bytes 184328 | tf_op jit(solution)/shard_map/ppermute | solution.py:153
  305.2 14.2 %collective-permute-start.3 = (f32[96,5,32]{2,1,0:T(8,128)S(1)}, f32[96,5,32]{2,1,0:T(8,128)S(1)}, u32[]{:S(2)}, u32[]{:S(2)}) collective-permute-start(f32[96,5,32]{2,1,0:T(8,128)S(1)} %get-tuple-element.30), channel_id=1, source_target_pairs={{1,0},{2,1},{3,2},{4,3},{5,4},{6,5},{7,6},{8,7},{9,8},{10,9},{11,1... | collective-permute-start | bytes 184328 | tf_op jit(solution)/shard_map/ppermute | solution.py:150
  319.3 1.3 copy-start.4
  319.4 1.3 copy-start.17
  334.0 1.3 copy-start.7
  337.5 0.9 copy-start.35
  337.6 1.6 copy-start.10
  338.4 1.8 copy-start.30
  341.0 41.2 %collective-permute-start.4 = (f32[96,5,32]{2,1,0:T(8,128)}, f32[96,5,32]{2,1,0:T(8,128)}, u32[]{:S(2)}, u32[]{:S(2)}) collective-permute-start(f32[96,5,32]{2,1,0:T(8,128)} %get-tuple-element.25), channel_id=1, source_target_pairs={{0,1},{1,2},{2,3},{3,4},{4,5},{5,6},{6,7},{7,8},{8,9},{9,10},{10,1... | collective-permute-start | bytes 184328 | tf_op jit(solution)/shard_map/ppermute | solution.py:153
  362.4 21.7 %all-to-all-start.2 = ((f32[128,1,320]{2,1,0:T(1,128)}), f32[128,1,320]{2,1,0:T(1,128)S(1)}, u32[]{:S(2)}, u32[]{:S(2)}) async-start(f32[128,1,320]{2,1,0:T(1,128)} %reshape.233), calls=%async_computation.2 | async-start | bytes 393216 | tf_op jit(solution)/shard_map/all_to_all | solution.py:218
  372.5 9.8 %copy-start.25 = (f32[96,8,96]{2,1,0:T(8,128)S(1)}, f32[96,8,96]{2,1,0:T(8,128)}, u32[]{:S(2)}) copy-start(f32[96,8,96]{2,1,0:T(8,128)} %get-tuple-element.27) | copy-start | bytes 884740
  375.2 88.7 %collective-permute-start.5 = (f32[96,5,32]{2,1,0:T(8,128)}, f32[96,5,32]{2,1,0:T(8,128)}, u32[]{:S(2)}, u32[]{:S(2)}) collective-permute-start(f32[96,5,32]{2,1,0:T(8,128)} %get-tuple-element.26), channel_id=1, source_target_pairs={{1,0},{2,1},{3,2},{4,3},{5,4},{6,5},{7,6},{8,7},{9,8},{10,9},{11,1... | collective-permute-start | bytes 184328 | tf_op jit(solution)/shard_map/ppermute | solution.py:150
  397.6 18.9 %copy-start.40 = (pred[256]{0:T(512)(128)(4,1)S(1)}, pred[256]{0:T(512)(128)(4,1)}, u32[]{:S(2)}) copy-start(pred[256]{0:T(512)(128)(4,1)} %copy-done.39) | copy-start | bytes 772
  397.6 21.5 %copy-start.38 = (f32[1,5,5,256]{3,0,2,1:T(1,128)S(1)}, f32[1,5,5,256]{3,0,2,1:T(1,128)}, u32[]{:S(2)}) copy-start(f32[1,5,5,256]{3,0,2,1:T(1,128)} %param.14) | copy-start | bytes 76804
  397.6 29.9 %copy-start.26 = (f32[96,5,128]{2,0,1:T(8,128)S(1)}, f32[96,5,128]{2,0,1:T(8,128)}, u32[]{:S(2)}) copy-start(f32[96,5,128]{2,0,1:T(8,128)} %copy.156) | copy-start | bytes 737284
  421.7 15.6 %all-to-all-start.3 = ((f32[5,128,2]{0,2,1:T(2,128)}), f32[5,128,2]{0,2,1:T(2,128)}, u32[]{:S(2)}, u32[]{:S(2)}) async-start(f32[5,128,2]{0,2,1:T(2,128)} %broadcast_select_fusion), calls=%async_computation.3 | async-start | bytes 262144 | tf_op jit(solution)/shard_map/all_to_all | solution.py:26
  441.3 2.9 copy-start.33
  459.5 15.0 %all-to-all-start.4 = ((f32[128,1,320]{2,1,0:T(1,128)}), f32[128,1,320]{2,1,0:T(1,128)S(1)}, u32[]{:S(2)}, u32[]{:S(2)}) async-start(f32[128,1,320]{2,1,0:T(1,128)} %reshape.235), calls=%async_computation.4 | async-start | bytes 393216 | tf_op jit(solution)/shard_map/all_to_all | solution.py:213
  464.0 1.5 copy-start.5
  494.1 1.0 copy-start.19
  494.1 1.1 copy-start.20
  494.1 1.4 copy-start.23
  494.2 1.5 copy-start.24
  494.3 0.8 copy-start.14
  508.8 1.2 copy-start.11
  510.0 0.9 copy-start.28
  510.0 9.9 %copy-start.2 = (f32[96,5,5,128]{3,2,1,0:T(8,128)S(1)}, f32[96,5,5,128]{3,2,1,0:T(8,128)}, u32[]{:S(2)}) copy-start(f32[96,5,5,128]{3,2,1,0:T(8,128)} %copy-done) | copy-start | bytes 3686404
  511.0 16.3 %collective-permute-start.6 = (f32[96,5,32]{2,1,0:T(8,128)S(1)}, f32[96,5,32]{2,1,0:T(8,128)S(1)}, u32[]{:S(2)}, u32[]{:S(2)}) collective-permute-start(f32[96,5,32]{2,1,0:T(8,128)S(1)} %get-tuple-element.21), channel_id=1, source_target_pairs={{0,1},{1,2},{2,3},{3,4},{4,5},{5,6},{6,7},{7,8},{8,9},{9,10},{10,1... | collective-permute-start | bytes 184328 | tf_op jit(solution)/shard_map/ppermute | solution.py:153
  513.3 14.1 %collective-permute-start.7 = (f32[96,5,32]{2,1,0:T(8,128)S(1)}, f32[96,5,32]{2,1,0:T(8,128)S(1)}, u32[]{:S(2)}, u32[]{:S(2)}) collective-permute-start(f32[96,5,32]{2,1,0:T(8,128)S(1)} %get-tuple-element.22), channel_id=1, source_target_pairs={{1,0},{2,1},{3,2},{4,3},{5,4},{6,5},{7,6},{8,7},{9,8},{10,9},{11,1... | collective-permute-start | bytes 184328 | tf_op jit(solution)/shard_map/ppermute | solution.py:150
  520.6 7.1 %copy-start.6 = (f32[96,25,128]{2,0,1:T(8,128)S(1)}, f32[96,25,128]{2,0,1:T(8,128)}, u32[]{:S(2)}) copy-start(f32[96,25,128]{2,0,1:T(8,128)} %copy-done.3) | copy-start | bytes 3686404
  527.7 1.0 copy-start.15
  544.3 0.9 copy-start.36

commit v3 on v2

--- a/solution.py
+++ b/solution.py
@@ -218,22 +218,37 @@
         received = lax.all_to_all(scatter_grid(grid, n_bx, n_by, ca, cb, width), AXES, 0, 0, tiled=True)
         return from_slices(received, ca, cb)
 
+    span = count * count
+    sweep_rows = to_z(
+        jnp.concatenate(
+            [
+                jnp.swapaxes(inverses, 0, 1).reshape(span, ca, cb, nz),
+                jnp.swapaxes(couplings[0::2][:2], 1, 2).astype(jnp.float32).reshape(2 * span, ca, cb, nz),
+            ],
+            axis=0,
+        ),
+        skew_big,
+    )
     base = adjoint_source - interface(initial, *tables)
-    packed = jnp.concatenate(
-        [
-            jnp.swapaxes(inverses, 0, 1).reshape(count * count, ca, cb, nz),
-            jnp.swapaxes(couplings, 1, 2).astype(jnp.float32).reshape(6 * count * count, ca, cb, nz),
-            base,
-            initial,
-        ],
-        axis=0,
+    other_rows = to_z(
+        jnp.concatenate(
+            [
+                jnp.swapaxes(couplings[jnp.array([1, 3, 4, 5])], 1, 2).astype(jnp.float32).reshape(4 * span, ca, cb, nz),
+                base,
+                initial,
+            ],
+            axis=0,
+        ),
+        skew_big,
     )
-    rows = to_z(packed, skew_big)
-    span = count * count
-    inv = as_matrices(rows[:, :span], count)
-    ks = [as_matrices(rows[:, span * (k + 1) : span * (k + 2)], count) for k in range(6)]
-    base_z = as_vectors(rows[:, 7 * span : 7 * span + count])
-    iterate = as_vectors(rows[:, 7 * span + count : 7 * span + 2 * count])
+    inv = as_matrices(sweep_rows[:, :span], count)
+    ks = [None] * 6
+    ks[0] = as_matrices(sweep_rows[:, span : 2 * span], count)
+    ks[2] = as_matrices(sweep_rows[:, 2 * span : 3 * span], count)
+    for place, k in enumerate((1, 3, 4, 5)):
+        ks[k] = as_matrices(other_rows[:, span * place : span * (place + 1)], count)
+    base_z = as_vectors(other_rows[:, 4 * span : 4 * span + count])
+    iterate = as_vectors(other_rows[:, 4 * span + count : 4 * span + 2 * count])
 
     for number in range(ITERS):
         if number > 0:

time: 600 us -> 516 us (0.86)
  waiting for transfers between devices: 134 us -> 79.5 us
  local copies, waits for them, and re-layouts: 239 us -> 210 us
    all_to_all x2 -> x3, waiting for transfers between devices: 106 us -> 53.9 us  [to_z(): lax.all_to_all(to_slices(values, devices), AXES, 0, 0, tiled=True)]
    reshape x3 -> x2, local copies, waits for them, and re-layouts: 18 us -> 8.02 us  [to_slices(): return shaped.reshape(devices, nz // devices * ca * cb, count)]
    ppermute x4, starting transfers between devices: 36.2 us -> 27.2 us  [shift_z(): lax.ppermute(values[:, :count, :nx], AXES, [(i + 1, i) for i in range(dev...]
    reshape x4, local copies, waits for them, and re-layouts: 31.7 us -> 23.8 us  [gather_grid(): return shaped.reshape(n_by * cb, count, width * n_bx * ca)]
    transpose x2 -> x3, other arithmetic: 12.3 us -> 5.36 us  [to_slices(): shaped = jnp.transpose(values, (3, 1, 2, 0))]
    all_to_all x2 -> x3, starting transfers between devices: 10.5 us -> 16.6 us  [to_z(): lax.all_to_all(to_slices(values, devices), AXES, 0, 0, tiled=True)]
    pallas_call x1 -> x2, Pallas kernels: 13.8 us -> 18.6 us  [skew_big(): pl.pallas_call(functools.partial(skew_kernel, nx=nx), out_shape=jax.Shape...]
    transpose x1 -> x2, local copies, waits for them, and re-layouts: 12 us -> 9.31 us  [gather_grid(): shaped = jnp.transpose(shaped, (1, 4, 5, 2, 0, 3))]
  transfers between devices with their start and end apart: 13 -> 14, of which waited for: 6 -> 7; matrix products, arithmetic and copies ran while one was open for 19% -> 30% of each run, Pallas kernels for 0% -> 2%
where the time goes in v3:
time: 516 us; the launch traced here: 506 us
  local copies, waits for them, and re-layouts  210 us (41%)
  waiting for transfers between devices  79.5 us (15%)
  starting transfers between devices  78.8 us (15%)
  Pallas kernels  66.8 us (13%)
  other arithmetic  50.4 us (10%)
  blocking collectives  19.4 us (4%)
    all_to_all x3, waiting for transfers between devices, to_z(): lax.all_to_all(to_slices(values, devices), AXES, 0, 0, tiled=True)  53.9 us
    pallas_call x4, Pallas kernels, sweep(): pl.pallas_call(kernel, out_shape=jax.ShapeDtypeStruct(rhs.shape, jnp.floa...  48.2 us
    ppermute x4, starting transfers between devices, shift_z(): lax.ppermute(values[:, :count, :nx], AXES, [(i + 1, i) for i in range(dev...  27.2 us
    reshape x4, local copies, waits for them, and re-layouts, gather_grid(): return shaped.reshape(n_by * cb, count, width * n_bx * ca)  23.8 us
    transpose x2, local copies, waits for them, and re-layouts, from_slices(): return jnp.transpose(shaped, (3, 1, 2, 0))  20.1 us
    all_to_all x1, blocking collectives, to_xy(): lax.all_to_all(scatter_grid(grid, n_bx, n_by, ca, cb, width), AXES, 0, 0,...  19.4 us
    pallas_call x2, Pallas kernels, skew_big(): pl.pallas_call(functools.partial(skew_kernel, nx=nx), out_shape=jax.Shape...  18.6 us
    unnamed x95, local copies, waits for them, and re-layouts  17.6 us
  transfers between devices with their start and end apart: 14, of which 7 were waited for; matrix products, arithmetic and copies ran while one was open for 30% of the time, Pallas kernels for 2%

profile of v3, /device:TPU:1, one launch (start us, length us, event | category | flops | bytes accessed | tf_op | source)
XLA Modules:
  0.0 506.1 jit_solution(13628129822341752631)
XLA Ops:
  2.7 3.6 copy.125
  6.3 3.1 gather_fusion.1
  12.0 11.5 %all-to-all-start = ((f32[5,128,2]{0,2,1:T(2,128)}), f32[5,128,2]{0,2,1:T(2,128)S(1)}, u32[]{:S(2)}, u32[]{:S(2)}) async-start(f32[5,128,2]{0,2,1:T(2,128)} %broadcast_select_fusion.1), calls=%async_computation | async-start | bytes 262144 | tf_op jit(solution)/shard_map/all_to_all | solution.py:26
  25.9 4.7 copy.135
  30.6 2.9 all-to-all-done
  33.5 7.3 %all-to-all-start.2 = ((f32[128,64,75]{2,1,0:T(8,128)}), f32[128,64,75]{2,1,0:T(8,128)}, u32[]{:S(2)}, u32[]{:S(2)}) async-start(f32[128,64,75]{2,1,0:T(8,128)} %bitcast.110), calls=%async_computation.2 | async-start | bytes 8388608 | tf_op jit(solution)/shard_map/all_to_all | solution.py:213
  40.9 3.7 gather_fusion
  45.7 3.6 scatter_custom_fusion
  49.3 2.9 copy.128
  53.2 3.5 maximum_bitcast_fusion
  56.7 7.3 %copy.129 = f32[512,4,4,110]{3,2,1,0:T(4,128)} copy(f32[512,4,4,110]{0,2,1,3:T(4,128)} %maximum_bitcast_fusion) | data formatting | bytes 7208960 | tf_op jit(solution)/shard_map/transpose | solution.py:33
  64.0 29.2 %all-to-all-done.2 = f32[128,64,75]{2,1,0:T(8,128)} async-done(((f32[128,64,75]{2,1,0:T(8,128)}), f32[128,64,75]{2,1,0:T(8,128)}, u32[]{:S(2)}, u32[]{:S(2)}) %all-to-all-start.2) | async-done | bytes 2457632 | tf_op jit(solution)/shard_map/all_to_all | solution.py:213
  93.2 5.0 all-to-all-start.1
  98.4 4.7 copy.136
  103.1 4.7 copy.137
  107.7 5.2 %copy.138.grid_ref = f32[64,75,128]{2,1,0:T(8,128)} copy(f32[64,75,128]{1,2,0:T(8,128)} %bitcast.116) | data formatting | bytes 4915200 | tf_op jit(solution)/shard_map/reshape | solution.py:41
  112.9 8.6 %shard_map.92 = f32[96,75,128]{2,1,0:T(8,128)} custom-call(f32[64,75,128]{2,1,0:T(8,128)} %copy.138.grid_ref), custom_call_target="tpu_custom_call" | custom-call | tf_op jit(solution)/shard_map/pallas_call | solution.py:98
  121.5 3.2 fusion.26
  133.9 16.5 %all-to-all-done.1 = f32[128,64,110]{2,1,0:T(8,128)} async-done(((f32[128,64,110]{2,1,0:T(8,128)}), f32[128,64,110]{2,1,0:T(8,128)}, u32[]{:S(2)}, u32[]{:S(2)}) %all-to-all-start.1) | async-done | bytes 3604512 | tf_op jit(solution)/shard_map/all_to_all | solution.py:213
  150.3 4.6 copy.130
  155.0 4.7 copy.131
  159.6 5.6 %copy.132.grid_ref = f32[64,110,128]{2,1,0:T(8,128)} copy(f32[64,110,128]{1,2,0:T(8,128)} %bitcast.117) | data formatting | bytes 7208960 | tf_op jit(solution)/shard_map/reshape | solution.py:41
  165.3 10.0 %shard_map.91 = f32[96,110,128]{2,1,0:T(8,128)} custom-call(f32[64,110,128]{2,1,0:T(8,128)} %copy.132.grid_ref), custom_call_target="tpu_custom_call" | custom-call | tf_op jit(solution)/shard_map/pallas_call | solution.py:98
  178.2 4.2 fusion.24
  182.4 2.2 collective-permute-start
  184.5 6.7 %collective-permute-start.1 = (f32[96,5,32]{2,1,0:T(8,128)S(1)}, f32[96,5,32]{2,1,0:T(8,128)S(1)}, u32[]{:S(2)}, u32[]{:S(2)}) collective-permute-start(f32[96,5,32]{2,1,0:T(8,128)S(1)} %get-tuple-element.13), channel_id=1, source_target_pairs={{1,0},{2,1},{3,2},{4,3},{5,4},{6,5},{7,6},{8,7},{9,8},{10,9},{11,1... | collective-permute-start | bytes 184328 | tf_op jit(solution)/shard_map/ppermute | solution.py:150
  194.3 1.9 fusion.27
  201.5 12.0 %shard_map.93 = f32[96,8,128]{2,1,0:T(8,128)} custom-call(f32[96,8,128]{2,1,0:T(8,128)} %copy_subtract_fusion.6.rhs_ref, f32[96,5,8,128]{3,2,1,0:T(8,128)} %pad.85.kx_ref, f32[96,5,8,128]{3,2,1,0:T(8,128)} %pad.93.ky_ref, f32[96,5,8,128]{3,2,1,0:T(8,128)} %pad.94.inv_ref), custom_call_target="tpu_custom_call" | custom-call | tf_op jit(solution)/shard_map/pallas_call | solution.py:187
  215.4 2.1 collective-permute-start.2
  218.0 7.0 %collective-permute-start.3 = (f32[96,5,32]{2,1,0:T(8,128)S(1)}, f32[96,5,32]{2,1,0:T(8,128)S(1)}, u32[]{:S(2)}, u32[]{:S(2)}) collective-permute-start(f32[96,5,32]{2,1,0:T(8,128)S(1)} %get-tuple-element.30), channel_id=1, source_target_pairs={{1,0},{2,1},{3,2},{4,3},{5,4},{6,5},{7,6},{8,7},{9,8},{10,9},{11,1... | collective-permute-start | bytes 184328 | tf_op jit(solution)/shard_map/ppermute | solution.py:150
  224.9 6.9 %collective-permute-done.2 = f32[96,5,32]{2,1,0:T(8,128)S(1)} collective-permute-done((f32[96,5,32]{2,1,0:T(8,128)S(1)}, f32[96,5,32]{2,1,0:T(8,128)S(1)}, u32[]{:S(2)}, u32[]{:S(2)}) %collective-permute-start.2) | collective-permute-done | bytes 61472 | tf_op jit(solution)/shard_map/ppermute | solution.py:153
  234.7 12.0 %shard_map.94 = f32[96,8,128]{2,1,0:T(8,128)} custom-call(f32[96,8,128]{2,1,0:T(8,128)} %copy_subtract_fusion.4.rhs_ref, f32[96,5,8,128]{3,2,1,0:T(8,128)} %get-tuple-element.19.kx_ref, f32[96,5,8,128]{3,2,1,0:T(8,128)} %get-tuple-element.17.ky_ref, f32[96,5,8,128]{3,2,1,0:T(8,128)} %pad.94.inv_ref), custom_call_target="tpu_custom_call" | custom-call | tf_op jit(solution)/shard_map/pallas_call | solution.py:187
  253.7 1.9 collective-permute-start.4
  255.7 7.3 %reshape.195 = f32[16,4,5,4,8,4]{5,4,3,1,0,2:T(8,128)} reshape(f32[64,5,128]{2,0,1:T(8,128)S(1)} %copy.159) | data formatting | bytes 327680 | tf_op jit(solution)/shard_map/reshape | solution.py:46
  263.0 7.9 %copy.160 = f32[8,16,4,4,4,5]{1,0,4,3,2,5:T(8,128)} copy(f32[8,16,4,4,4,5]{3,0,2,4,1,5:T(8,128)} %bitcast.106) | data formatting | bytes 327680 | tf_op jit(solution)/shard_map/transpose | solution.py:47
  273.6 2.0 reshape.265
  275.6 9.4 %all-to-all-start.3 = ((f32[128,1,320]{2,1,0:T(1,128)}), f32[128,1,320]{2,1,0:T(1,128)S(1)}, u32[]{:S(2)}, u32[]{:S(2)}) async-start(f32[128,1,320]{2,1,0:T(1,128)} %reshape.265), calls=%async_computation.3 | async-start | bytes 393216 | tf_op jit(solution)/shard_map/all_to_all | solution.py:218
  285.0 2.8 multiply_reduce_fusion.3
  287.7 7.0 %collective-permute-start.5 = (f32[96,5,32]{2,1,0:T(8,128)}, f32[96,5,32]{2,1,0:T(8,128)}, u32[]{:S(2)}, u32[]{:S(2)}) collective-permute-start(f32[96,5,32]{2,1,0:T(8,128)} %get-tuple-element.26), channel_id=1, source_target_pairs={{1,0},{2,1},{3,2},{4,3},{5,4},{6,5},{7,6},{8,7},{9,8},{10,9},{11,1... | collective-permute-start | bytes 184328 | tf_op jit(solution)/shard_map/ppermute | solution.py:150
  299.0 1.8 reshape.266
  301.9 7.7 %reshape.197 = f32[512,4,4,5]{2,1,0,3:T(4,128)} reshape(f32[128,64,5]{1,0,2:T(8,128)S(1)} %copy.162) | data formatting | bytes 327680 | tf_op jit(solution)/shard_map/reshape | solution.py:54
  309.6 15.4 %copy.163 = f32[5,4,4,512]{0,3,2,1:T(8,128)} copy(f32[5,4,4,512]{2,1,3,0:T(4,128)} %bitcast.107) | data formatting | bytes 327680 | tf_op jit(solution)/shard_map/transpose | solution.py:55
  325.0 3.7 gather_fusion.2
  333.9 5.7 %all-to-all-start.4 = ((f32[5,128,2]{0,2,1:T(2,128)}), f32[5,128,2]{0,2,1:T(2,128)}, u32[]{:S(2)}, u32[]{:S(2)}) async-start(f32[5,128,2]{0,2,1:T(2,128)} %broadcast_select_fusion), calls=%async_computation.4 | async-start | bytes 262144 | tf_op jit(solution)/shard_map/all_to_all | solution.py:26
  340.5 9.0 %all-to-all-done.4 = f32[5,128,2]{0,2,1:T(2,128)} async-done(((f32[5,128,2]{0,2,1:T(2,128)}), f32[5,128,2]{0,2,1:T(2,128)}, u32[]{:S(2)}, u32[]{:S(2)}) %all-to-all-start.4) | async-done | bytes 5152 | tf_op jit(solution)/shard_map/all_to_all | solution.py:26
  349.5 4.0 scatter_custom_fusion.1
  353.5 3.0 copy.166
  357.3 4.6 copy.167
  361.8 7.0 %reshape.200 = f32[128,64,5]{1,0,2:T(8,128)S(1)} reshape(f32[512,4,4,5]{2,1,0,3:T(4,128)} %copy.167) | data formatting | bytes 327680 | tf_op jit(solution)/shard_map/reshape | solution.py:34
  369.9 2.0 reshape.267
  371.8 4.2 all-to-all-start.5
  378.5 8.2 %all-to-all-done.5 = f32[128,1,320]{2,1,0:T(1,128)S(1)} async-done(((f32[128,1,320]{2,1,0:T(1,128)}), f32[128,1,320]{2,1,0:T(1,128)S(1)}, u32[]{:S(2)}, u32[]{:S(2)}) %all-to-all-start.5) | async-done | bytes 163872 | tf_op jit(solution)/shard_map/all_to_all | solution.py:213
  393.0 7.4 %copy.185 = f32[16,4,5,4,8,4]{5,4,3,2,1,0:T(8,128)} copy(f32[16,4,5,4,8,4]{0,4,1,5,3,2:T(8,128)} %bitcast.120) | data formatting | bytes 327680 | tf_op jit(solution)/shard_map/reshape | solution.py:41
  400.4 5.6 %reshape.258 = f32[64,5,128]{2,1,0:T(8,128)S(1)} reshape(f32[16,4,5,4,8,4]{5,4,3,2,1,0:T(8,128)} %copy.185) | data formatting | bytes 327680 | tf_op jit(solution)/shard_map/reshape | solution.py:41
  409.1 12.0 %shard_map.95 = f32[96,8,128]{2,1,0:T(8,128)} custom-call(f32[96,8,128]{2,1,0:T(8,128)} %copy_subtract_fusion.2.rhs_ref, f32[96,5,8,128]{3,2,1,0:T(8,128)} %pad.85.kx_ref, f32[96,5,8,128]{3,2,1,0:T(8,128)} %pad.93.ky_ref, f32[96,5,8,128]{3,2,1,0:T(8,128)} %pad.94.inv_ref), custom_call_target="tpu_custom_call" | custom-call | tf_op jit(solution)/shard_map/pallas_call | solution.py:187
  423.3 2.3 collective-permute-start.6
  425.6 6.6 %collective-permute-start.7 = (f32[96,5,32]{2,1,0:T(8,128)S(1)}, f32[96,5,32]{2,1,0:T(8,128)S(1)}, u32[]{:S(2)}, u32[]{:S(2)}) collective-permute-start(f32[96,5,32]{2,1,0:T(8,128)S(1)} %get-tuple-element.22), channel_id=1, source_target_pairs={{1,0},{2,1},{3,2},{4,3},{5,4},{6,5},{7,6},{8,7},{9,8},{10,9},{11,1... | collective-permute-start | bytes 184328 | tf_op jit(solution)/shard_map/ppermute | solution.py:150
  432.9 6.8 %collective-permute-done.6 = f32[96,5,32]{2,1,0:T(8,128)S(1)} collective-permute-done((f32[96,5,32]{2,1,0:T(8,128)S(1)}, f32[96,5,32]{2,1,0:T(8,128)S(1)}, u32[]{:S(2)}, u32[]{:S(2)}) %collective-permute-start.6) | collective-permute-done | bytes 61472 | tf_op jit(solution)/shard_map/ppermute | solution.py:153
  442.2 12.2 %shard_map.96 = f32[96,8,128]{2,1,0:T(8,128)} custom-call(f32[96,8,128]{2,1,0:T(8,128)} %copy_subtract_fusion.rhs_ref, f32[96,5,8,128]{3,2,1,0:T(8,128)} %get-tuple-element.19.kx_ref, f32[96,5,8,128]{3,2,1,0:T(8,128)} %get-tuple-element.17.ky_ref, f32[96,5,8,128]{3,2,1,0:T(8,128)} %pad.94.inv_ref), custom_call_target="tpu_custom_call" | custom-call | tf_op jit(solution)/shard_map/pallas_call | solution.py:187
  457.6 6.9 %reshape.203 = f32[16,4,5,4,8,4]{5,4,3,1,0,2:T(8,128)} reshape(f32[64,5,128]{2,0,1:T(8,128)S(1)} %copy.180) | data formatting | bytes 327680 | tf_op jit(solution)/shard_map/reshape | solution.py:46
  464.5 7.3 %copy.181 = f32[8,16,4,4,4,5]{1,0,4,3,2,5:T(8,128)S(1)} copy(f32[8,16,4,4,4,5]{3,0,2,4,1,5:T(8,128)} %bitcast.108) | data formatting | bytes 327680 | tf_op jit(solution)/shard_map/transpose | solution.py:47
  472.7 19.4 %all_to_all.43 = f32[128,1,320]{2,1,0:T(1,128)S(1)} all-to-all(f32[128,1,320]{2,1,0:T(1,128)S(1)} %reshape.269), channel_id=1, replica_groups=mesh['bx'=8,'by'=16] {'bx','by'}, dimensions={0} | all-to-all | bytes 327680 | tf_op jit(solution)/shard_map/all_to_all | solution.py:218
  493.4 7.7 %reshape.205 = f32[512,4,4,5]{2,1,0,3:T(4,128)} reshape(f32[128,64,5]{1,0,2:T(8,128)S(1)} %copy.183) | data formatting | bytes 327680 | tf_op jit(solution)/shard_map/reshape | solution.py:54
  501.1 4.8 copy.184
  (246 shorter events, 80.2 us)
Async XLA Ops:
  1.9 4.4 copy-start.39
  2.7 8.4 %copy-start.30 = (pred[128,2]{1,0:T(8,128)(4,1)}, pred[128,2]{1,0:T(8,128)(4,1)S(1)}, u32[]{:S(2)}) copy-start(pred[128,2]{1,0:T(8,128)(4,1)S(1)} %fusion.17) | copy-start | bytes 772
  2.7 20.8 %copy-start.26 = (f32[5,5,4,4,512]{4,3,2,1,0:T(4,128)S(1)}, f32[5,5,4,4,512]{4,3,2,1,0:T(4,128)}, u32[]{:S(2)}) copy-start(f32[5,5,4,4,512]{4,3,2,1,0:T(4,128)} %param.13) | copy-start | bytes 2457604
  6.3 17.2 %copy-start.17 = (bf16[6,5,5,4,4,512]{5,4,3,2,1,0:T(4,128)(2,1)S(1)}, bf16[6,5,5,4,4,512]{5,4,3,2,1,0:T(4,128)(2,1)}, u32[]{:S(2)}) copy-start(bf16[6,5,5,4,4,512]{5,4,3,2,1,0:T(4,128)(2,1)} %param.14) | copy-start | bytes 7372804
  12.0 21.5 %all-to-all-start = ((f32[5,128,2]{0,2,1:T(2,128)}), f32[5,128,2]{0,2,1:T(2,128)S(1)}, u32[]{:S(2)}, u32[]{:S(2)}) async-start(f32[5,128,2]{0,2,1:T(2,128)} %broadcast_select_fusion.1), calls=%async_computation | async-start | bytes 262144 | tf_op jit(solution)/shard_map/all_to_all | solution.py:26
  33.5 7.3 %copy-start.43 = (s32[4]{0:T(128)S(1)}, s32[4]{0:T(128)}, u32[]{:S(2)}) copy-start(s32[4]{0:T(128)} %constant.194) | copy-start | bytes 52
  33.5 59.7 %all-to-all-start.2 = ((f32[128,64,75]{2,1,0:T(8,128)}), f32[128,64,75]{2,1,0:T(8,128)}, u32[]{:S(2)}, u32[]{:S(2)}) async-start(f32[128,64,75]{2,1,0:T(8,128)} %bitcast.110), calls=%async_computation.2 | async-start | bytes 8388608 | tf_op jit(solution)/shard_map/all_to_all | solution.py:213
  45.0 0.7 copy-start.41
  45.7 3.6 copy-start.42
  93.2 57.2 %all-to-all-start.1 = ((f32[128,64,110]{2,1,0:T(8,128)}), f32[128,64,110]{2,1,0:T(8,128)}, u32[]{:S(2)}, u32[]{:S(2)}) async-start(f32[128,64,110]{2,1,0:T(8,128)} %bitcast.115), calls=%async_computation.1 | async-start | bytes 8388608 | tf_op jit(solution)/shard_map/all_to_all | solution.py:213
  98.2 152.2 %copy-start.32 = (s32[128]{0:T(128)}, s32[128]{0:T(128)S(1)}, u32[]{:S(2)}) copy-start(s32[128]{0:T(128)S(1)} %broadcast_add_fusion) | copy-start | bytes 1540
  98.2 152.2 %copy-start.34 = (s32[128]{0:T(128)}, s32[128]{0:T(128)S(1)}, u32[]{:S(2)}) copy-start(s32[128]{0:T(128)S(1)} %iota_and_fusion) | copy-start | bytes 1540
  98.3 152.1 %copy-start.36 = (pred[128]{0:T(512)(128)(4,1)}, pred[128]{0:T(512)(128)(4,1)S(1)}, u32[]{:S(2)}) copy-start(pred[128]{0:T(512)(128)(4,1)S(1)} %compare_and_fusion.1) | copy-start | bytes 388
  98.3 152.2 %copy-start.28 = (pred[96,5,128]{2,1,0:T(8,128)(4,1)}, pred[96,5,128]{2,1,0:T(8,128)(4,1)S(1)}, u32[]{:S(2)}) copy-start(pred[96,5,128]{2,1,0:T(8,128)(4,1)S(1)} %fusion.12) | copy-start | bytes 184324
  98.4 119.1 %copy-start.24 = (pred[96,8,128]{2,1,0:T(8,128)(4,1)}, pred[96,8,128]{2,1,0:T(8,128)(4,1)S(1)}, u32[]{:S(2)}) copy-start(pred[96,8,128]{2,1,0:T(8,128)(4,1)S(1)} %get-tuple-element.35) | copy-start | bytes 294916
  130.5 2.0 copy-start
  177.9 22.4 %copy-start.15 = (f32[96,5,128]{2,1,0:T(8,128)}, f32[96,5,128]{2,1,0:T(8,128)S(1)}, u32[]{:S(2)}) copy-start(f32[96,5,128]{2,1,0:T(8,128)S(1)} %get-tuple-element.6) | copy-start | bytes 737284
  182.4 17.2 %collective-permute-start = (f32[96,5,32]{2,1,0:T(8,128)S(1)}, f32[96,5,32]{2,1,0:T(8,128)S(1)}, u32[]{:S(2)}, u32[]{:S(2)}) collective-permute-start(f32[96,5,32]{2,1,0:T(8,128)S(1)} %get-tuple-element.12), channel_id=1, source_target_pairs={{0,1},{1,2},{2,3},{3,4},{4,5},{5,6},{6,7},{7,8},{8,9},{9,10},{10,1... | collective-permute-start | bytes 184328 | tf_op jit(solution)/shard_map/ppermute | solution.py:153
  184.5 15.3 %collective-permute-start.1 = (f32[96,5,32]{2,1,0:T(8,128)S(1)}, f32[96,5,32]{2,1,0:T(8,128)S(1)}, u32[]{:S(2)}, u32[]{:S(2)}) collective-permute-start(f32[96,5,32]{2,1,0:T(8,128)S(1)} %get-tuple-element.13), channel_id=1, source_target_pairs={{1,0},{2,1},{3,2},{4,3},{5,4},{6,5},{7,6},{8,7},{9,8},{10,9},{11,1... | collective-permute-start | bytes 184328 | tf_op jit(solution)/shard_map/ppermute | solution.py:150
  192.8 3.5 copy-start.8
  194.3 2.0 copy-start.9
  198.8 1.2 copy-start.3
  213.5 1.2 copy-start.12
  215.1 2.6 copy-start.1
  215.4 16.4 %collective-permute-start.2 = (f32[96,5,32]{2,1,0:T(8,128)S(1)}, f32[96,5,32]{2,1,0:T(8,128)S(1)}, u32[]{:S(2)}, u32[]{:S(2)}) collective-permute-start(f32[96,5,32]{2,1,0:T(8,128)S(1)} %get-tuple-element.29), channel_id=1, source_target_pairs={{0,1},{1,2},{2,3},{3,4},{4,5},{5,6},{6,7},{7,8},{8,9},{9,10},{10,1... | collective-permute-start | bytes 184328 | tf_op jit(solution)/shard_map/ppermute | solution.py:153
  218.0 14.2 %collective-permute-start.3 = (f32[96,5,32]{2,1,0:T(8,128)S(1)}, f32[96,5,32]{2,1,0:T(8,128)S(1)}, u32[]{:S(2)}, u32[]{:S(2)}) collective-permute-start(f32[96,5,32]{2,1,0:T(8,128)S(1)} %get-tuple-element.30), channel_id=1, source_target_pairs={{1,0},{2,1},{3,2},{4,3},{5,4},{6,5},{7,6},{8,7},{9,8},{10,9},{11,1... | collective-permute-start | bytes 184328 | tf_op jit(solution)/shard_map/ppermute | solution.py:150
  232.1 1.3 copy-start.4
  232.2 1.3 copy-start.16
  246.7 1.3 copy-start.7
  250.3 1.5 copy-start.10
  253.7 40.9 %collective-permute-start.4 = (f32[96,5,32]{2,1,0:T(8,128)}, f32[96,5,32]{2,1,0:T(8,128)}, u32[]{:S(2)}, u32[]{:S(2)}) collective-permute-start(f32[96,5,32]{2,1,0:T(8,128)} %get-tuple-element.25), channel_id=1, source_target_pairs={{0,1},{1,2},{2,3},{3,4},{4,5},{5,6},{6,7},{7,8},{8,9},{9,10},{10,1... | collective-permute-start | bytes 184328 | tf_op jit(solution)/shard_map/ppermute | solution.py:153
  275.6 21.0 %all-to-all-start.3 = ((f32[128,1,320]{2,1,0:T(1,128)}), f32[128,1,320]{2,1,0:T(1,128)S(1)}, u32[]{:S(2)}, u32[]{:S(2)}) async-start(f32[128,1,320]{2,1,0:T(1,128)} %reshape.265), calls=%async_computation.3 | async-start | bytes 393216 | tf_op jit(solution)/shard_map/all_to_all | solution.py:218
  284.9 9.7 %copy-start.22 = (f32[96,8,96]{2,1,0:T(8,128)S(1)}, f32[96,8,96]{2,1,0:T(8,128)}, u32[]{:S(2)}) copy-start(f32[96,8,96]{2,1,0:T(8,128)} %get-tuple-element.27) | copy-start | bytes 884740
  287.7 88.4 %collective-permute-start.5 = (f32[96,5,32]{2,1,0:T(8,128)}, f32[96,5,32]{2,1,0:T(8,128)}, u32[]{:S(2)}, u32[]{:S(2)}) collective-permute-start(f32[96,5,32]{2,1,0:T(8,128)} %get-tuple-element.26), channel_id=1, source_target_pairs={{1,0},{2,1},{3,2},{4,3},{5,4},{6,5},{7,6},{8,7},{9,8},{10,9},{11,1... | collective-permute-start | bytes 184328 | tf_op jit(solution)/shard_map/ppermute | solution.py:150
  309.6 19.1 %copy-start.40 = (pred[256]{0:T(512)(128)(4,1)S(1)}, pred[256]{0:T(512)(128)(4,1)}, u32[]{:S(2)}) copy-start(pred[256]{0:T(512)(128)(4,1)} %compare_and_fusion) | copy-start | bytes 772
  309.6 21.7 %copy-start.38 = (f32[1,5,5,256]{3,0,2,1:T(1,128)S(1)}, f32[1,5,5,256]{3,0,2,1:T(1,128)}, u32[]{:S(2)}) copy-start(f32[1,5,5,256]{3,0,2,1:T(1,128)} %param.15) | copy-start | bytes 76804
  309.6 22.5 %copy-start.31 = (pred[128,2]{1,0:T(8,128)(4,1)S(1)}, pred[128,2]{1,0:T(8,128)(4,1)}, u32[]{:S(2)}) copy-start(pred[128,2]{1,0:T(8,128)(4,1)} %copy-done.30) | copy-start | bytes 772
  309.6 30.0 %copy-start.23 = (f32[96,5,128]{2,0,1:T(8,128)S(1)}, f32[96,5,128]{2,0,1:T(8,128)}, u32[]{:S(2)}) copy-start(f32[96,5,128]{2,0,1:T(8,128)} %copy.172) | copy-start | bytes 737284
  333.9 15.6 %all-to-all-start.4 = ((f32[5,128,2]{0,2,1:T(2,128)}), f32[5,128,2]{0,2,1:T(2,128)}, u32[]{:S(2)}, u32[]{:S(2)}) async-start(f32[5,128,2]{0,2,1:T(2,128)} %broadcast_select_fusion), calls=%async_computation.4 | async-start | bytes 262144 | tf_op jit(solution)/shard_map/all_to_all | solution.py:26
  353.5 3.0 copy-start.27
  371.8 14.8 %all-to-all-start.5 = ((f32[128,1,320]{2,1,0:T(1,128)}), f32[128,1,320]{2,1,0:T(1,128)S(1)}, u32[]{:S(2)}, u32[]{:S(2)}) async-start(f32[128,1,320]{2,1,0:T(1,128)} %reshape.267), calls=%async_computation.5 | async-start | bytes 393216 | tf_op jit(solution)/shard_map/all_to_all | solution.py:213
  376.1 1.5 copy-start.5
  400.4 5.7 %copy-start.33 = (s32[128]{0:T(128)S(1)}, s32[128]{0:T(128)}, u32[]{:S(2)}) copy-start(s32[128]{0:T(128)} %copy-done.32) | copy-start | bytes 1540
  400.4 5.7 %copy-start.35 = (s32[128]{0:T(128)S(1)}, s32[128]{0:T(128)}, u32[]{:S(2)}) copy-start(s32[128]{0:T(128)} %copy-done.34) | copy-start | bytes 1540
  400.4 5.7 %copy-start.37 = (pred[128]{0:T(512)(128)(4,1)S(1)}, pred[128]{0:T(512)(128)(4,1)}, u32[]{:S(2)}) copy-start(pred[128]{0:T(512)(128)(4,1)} %copy-done.36) | copy-start | bytes 388
  406.4 1.0 copy-start.18
  406.4 1.1 copy-start.19
  406.4 1.4 copy-start.20
  406.4 1.5 copy-start.21
  406.6 0.7 copy-start.13
  421.1 1.2 copy-start.11
  422.2 0.9 copy-start.25
  422.3 9.9 %copy-start.2 = (f32[96,5,5,128]{3,2,1,0:T(8,128)S(1)}, f32[96,5,5,128]{3,2,1,0:T(8,128)}, u32[]{:S(2)}) copy-start(f32[96,5,5,128]{3,2,1,0:T(8,128)} %copy-done) | copy-start | bytes 3686404
  423.3 16.3 %collective-permute-start.6 = (f32[96,5,32]{2,1,0:T(8,128)S(1)}, f32[96,5,32]{2,1,0:T(8,128)S(1)}, u32[]{:S(2)}, u32[]{:S(2)}) collective-permute-start(f32[96,5,32]{2,1,0:T(8,128)S(1)} %get-tuple-element.21), channel_id=1, source_target_pairs={{0,1},{1,2},{2,3},{3,4},{4,5},{5,6},{6,7},{7,8},{8,9},{9,10},{10,1... | collective-permute-start | bytes 184328 | tf_op jit(solution)/shard_map/ppermute | solution.py:153
  425.6 14.1 %collective-permute-start.7 = (f32[96,5,32]{2,1,0:T(8,128)S(1)}, f32[96,5,32]{2,1,0:T(8,128)S(1)}, u32[]{:S(2)}, u32[]{:S(2)}) collective-permute-start(f32[96,5,32]{2,1,0:T(8,128)S(1)} %get-tuple-element.22), channel_id=1, source_target_pairs={{1,0},{2,1},{3,2},{4,3},{5,4},{6,5},{7,6},{8,7},{9,8},{10,9},{11,1... | collective-permute-start | bytes 184328 | tf_op jit(solution)/shard_map/ppermute | solution.py:150
  432.8 7.1 %copy-start.6 = (f32[96,25,128]{2,0,1:T(8,128)S(1)}, f32[96,25,128]{2,0,1:T(8,128)}, u32[]{:S(2)}) copy-start(f32[96,25,128]{2,0,1:T(8,128)} %copy-done.3) | copy-start | bytes 3686404
  440.0 1.0 copy-start.14
  456.6 0.9 copy-start.29

commit v4 on v3

--- a/solution.py
+++ b/solution.py
@@ -155,6 +155,13 @@
     return jnp.concatenate([halo, values[..., :-nx]], axis=-1)
 
 
+def tree_sum(terms):
+    while len(terms) > 1:
+        paired = [terms[i] + terms[i + 1] for i in range(0, len(terms) - 1, 2)]
+        terms = paired + terms[len(paired) * 2 :]
+    return terms[0]
+
+
 def sweep_kernel(rhs_ref, kx_ref, ky_ref, inv_ref, out_ref, *, forward, nx, count):
     steps = rhs_ref.shape[0]
     lanes = rhs_ref.shape[2]
@@ -169,12 +176,10 @@
     def step(s, fresh):
         t = s if forward else steps - 1 - s
         from_x = jnp.where(keep, pltpu.roll(fresh, shift, 1), 0.0)
-        right = rhs_ref[t]
-        for j in range(count):
-            right = right - kx_ref[t, j] * from_x[j : j + 1, :] - ky_ref[t, j] * fresh[j : j + 1, :]
-        result = inv_ref[t, 0] * right[0:1, :]
-        for j in range(1, count):
-            result = result + inv_ref[t, j] * right[j : j + 1, :]
+        terms = [kx_ref[t, j] * from_x[j : j + 1, :] for j in range(count)]
+        terms += [ky_ref[t, j] * fresh[j : j + 1, :] for j in range(count)]
+        right = rhs_ref[t] - tree_sum(terms)
+        result = tree_sum([inv_ref[t, j] * right[j : j + 1, :] for j in range(count)])
         out_ref[t] = result
         return result
 

time: 516 us -> 514 us (level)
  no operation moved by 1% of the time
where the time goes in v4:
time: 514 us; the launch traced here: 504 us
  local copies, waits for them, and re-layouts  210 us (41%)
  waiting for transfers between devices  79.5 us (15%)
  starting transfers between devices  78.8 us (15%)
  Pallas kernels  64.8 us (13%)
  other arithmetic  50.4 us (10%)
  blocking collectives  19.4 us (4%)
    all_to_all x3, waiting for transfers between devices, to_z(): lax.all_to_all(to_slices(values, devices), AXES, 0, 0, tiled=True)  53.9 us
    pallas_call x4, Pallas kernels, sweep(): pl.pallas_call(kernel, out_shape=jax.ShapeDtypeStruct(rhs.shape, jnp.floa...  46.2 us
    ppermute x4, starting transfers between devices, shift_z(): lax.ppermute(values[:, :count, :nx], AXES, [(i + 1, i) for i in range(dev...  27.2 us
    reshape x4, local copies, waits for them, and re-layouts, gather_grid(): return shaped.reshape(n_by * cb, count, width * n_bx * ca)  23.8 us
    transpose x2, local copies, waits for them, and re-layouts, from_slices(): return jnp.transpose(shaped, (3, 1, 2, 0))  20.1 us
    all_to_all x1, blocking collectives, to_xy(): lax.all_to_all(scatter_grid(grid, n_bx, n_by, ca, cb, width), AXES, 0, 0,...  19.4 us
    pallas_call x2, Pallas kernels, skew_big(): pl.pallas_call(functools.partial(skew_kernel, nx=nx), out_shape=jax.Shape...  18.6 us
    unnamed x95, local copies, waits for them, and re-layouts  17.6 us
  transfers between devices with their start and end apart: 14, of which 7 were waited for; matrix products, arithmetic and copies ran while one was open for 30% of the time, Pallas kernels for 2%

profile of v4, /device:TPU:1, one launch (start us, length us, event | category | flops | bytes accessed | tf_op | source)
XLA Modules:
  0.0 504.1 jit_solution(9102443166158619001)
XLA Ops:
  2.7 3.6 copy.125
  6.3 3.1 gather_fusion.1
  12.0 11.5 %all-to-all-start = ((f32[5,128,2]{0,2,1:T(2,128)}), f32[5,128,2]{0,2,1:T(2,128)S(1)}, u32[]{:S(2)}, u32[]{:S(2)}) async-start(f32[5,128,2]{0,2,1:T(2,128)} %broadcast_select_fusion.1), calls=%async_computation | async-start | bytes 262144 | tf_op jit(solution)/shard_map/all_to_all | solution.py:26
  25.9 4.7 copy.135
  30.6 2.9 all-to-all-done
  33.5 7.3 %all-to-all-start.2 = ((f32[128,64,75]{2,1,0:T(8,128)}), f32[128,64,75]{2,1,0:T(8,128)}, u32[]{:S(2)}, u32[]{:S(2)}) async-start(f32[128,64,75]{2,1,0:T(8,128)} %bitcast.110), calls=%async_computation.2 | async-start | bytes 8388608 | tf_op jit(solution)/shard_map/all_to_all | solution.py:218
  40.9 3.7 gather_fusion
  45.7 3.6 scatter_custom_fusion
  49.3 2.9 copy.128
  53.2 3.5 maximum_bitcast_fusion
  56.7 7.3 %copy.129 = f32[512,4,4,110]{3,2,1,0:T(4,128)} copy(f32[512,4,4,110]{0,2,1,3:T(4,128)} %maximum_bitcast_fusion) | data formatting | bytes 7208960 | tf_op jit(solution)/shard_map/transpose | solution.py:33
  64.0 29.2 %all-to-all-done.2 = f32[128,64,75]{2,1,0:T(8,128)} async-done(((f32[128,64,75]{2,1,0:T(8,128)}), f32[128,64,75]{2,1,0:T(8,128)}, u32[]{:S(2)}, u32[]{:S(2)}) %all-to-all-start.2) | async-done | bytes 2457632 | tf_op jit(solution)/shard_map/all_to_all | solution.py:218
  93.2 5.0 %all-to-all-start.1 = ((f32[128,64,110]{2,1,0:T(8,128)}), f32[128,64,110]{2,1,0:T(8,128)}, u32[]{:S(2)}, u32[]{:S(2)}) async-start(f32[128,64,110]{2,1,0:T(8,128)} %bitcast.115), calls=%async_computation.1 | async-start | bytes 8388608 | tf_op jit(solution)/shard_map/all_to_all | solution.py:218
  98.4 4.7 copy.136
  103.1 4.7 copy.137
  107.7 5.2 %copy.138.grid_ref = f32[64,75,128]{2,1,0:T(8,128)} copy(f32[64,75,128]{1,2,0:T(8,128)} %bitcast.116) | data formatting | bytes 4915200 | tf_op jit(solution)/shard_map/reshape | solution.py:41
  112.9 8.6 %shard_map.92 = f32[96,75,128]{2,1,0:T(8,128)} custom-call(f32[64,75,128]{2,1,0:T(8,128)} %copy.138.grid_ref), custom_call_target="tpu_custom_call" | custom-call | tf_op jit(solution)/shard_map/pallas_call | solution.py:98
  121.5 3.2 fusion.26
  133.9 16.5 %all-to-all-done.1 = f32[128,64,110]{2,1,0:T(8,128)} async-done(((f32[128,64,110]{2,1,0:T(8,128)}), f32[128,64,110]{2,1,0:T(8,128)}, u32[]{:S(2)}, u32[]{:S(2)}) %all-to-all-start.1) | async-done | bytes 3604512 | tf_op jit(solution)/shard_map/all_to_all | solution.py:218
  150.3 4.6 copy.130
  155.0 4.7 copy.131
  159.6 5.6 %copy.132.grid_ref = f32[64,110,128]{2,1,0:T(8,128)} copy(f32[64,110,128]{1,2,0:T(8,128)} %bitcast.117) | data formatting | bytes 7208960 | tf_op jit(solution)/shard_map/reshape | solution.py:41
  165.3 10.0 %shard_map.91 = f32[96,110,128]{2,1,0:T(8,128)} custom-call(f32[64,110,128]{2,1,0:T(8,128)} %copy.132.grid_ref), custom_call_target="tpu_custom_call" | custom-call | tf_op jit(solution)/shard_map/pallas_call | solution.py:98
  178.2 4.2 fusion.24
  182.4 2.2 collective-permute-start
  184.5 6.7 %collective-permute-start.1 = (f32[96,5,32]{2,1,0:T(8,128)S(1)}, f32[96,5,32]{2,1,0:T(8,128)S(1)}, u32[]{:S(2)}, u32[]{:S(2)}) collective-permute-start(f32[96,5,32]{2,1,0:T(8,128)S(1)} %get-tuple-element.13), channel_id=1, source_target_pairs={{1,0},{2,1},{3,2},{4,3},{5,4},{6,5},{7,6},{8,7},{9,8},{10,9},{11,1... | collective-permute-start | bytes 184328 | tf_op jit(solution)/shard_map/ppermute | solution.py:150
  194.3 1.9 fusion.27
  201.5 11.5 %shard_map.93 = f32[96,8,128]{2,1,0:T(8,128)} custom-call(f32[96,8,128]{2,1,0:T(8,128)} %copy_subtract_fusion.6.rhs_ref, f32[96,5,8,128]{3,2,1,0:T(8,128)} %pad.85.kx_ref, f32[96,5,8,128]{3,2,1,0:T(8,128)} %pad.93.ky_ref, f32[96,5,8,128]{3,2,1,0:T(8,128)} %pad.94.inv_ref), custom_call_target="tpu_custom_call" | custom-call | tf_op jit(solution)/shard_map/pallas_call | solution.py:192
  214.9 2.1 collective-permute-start.2
  217.5 7.0 %collective-permute-start.3 = (f32[96,5,32]{2,1,0:T(8,128)S(1)}, f32[96,5,32]{2,1,0:T(8,128)S(1)}, u32[]{:S(2)}, u32[]{:S(2)}) collective-permute-start(f32[96,5,32]{2,1,0:T(8,128)S(1)} %get-tuple-element.30), channel_id=1, source_target_pairs={{1,0},{2,1},{3,2},{4,3},{5,4},{6,5},{7,6},{8,7},{9,8},{10,9},{11,1... | collective-permute-start | bytes 184328 | tf_op jit(solution)/shard_map/ppermute | solution.py:150
  224.4 6.9 %collective-permute-done.2 = f32[96,5,32]{2,1,0:T(8,128)S(1)} collective-permute-done((f32[96,5,32]{2,1,0:T(8,128)S(1)}, f32[96,5,32]{2,1,0:T(8,128)S(1)}, u32[]{:S(2)}, u32[]{:S(2)}) %collective-permute-start.2) | collective-permute-done | bytes 61472 | tf_op jit(solution)/shard_map/ppermute | solution.py:153
  234.2 11.5 %shard_map.94 = f32[96,8,128]{2,1,0:T(8,128)} custom-call(f32[96,8,128]{2,1,0:T(8,128)} %copy_subtract_fusion.4.rhs_ref, f32[96,5,8,128]{3,2,1,0:T(8,128)} %get-tuple-element.19.kx_ref, f32[96,5,8,128]{3,2,1,0:T(8,128)} %get-tuple-element.17.ky_ref, f32[96,5,8,128]{3,2,1,0:T(8,128)} %pad.94.inv_ref), custom_call_target="tpu_custom_call" | custom-call | tf_op jit(solution)/shard_map/pallas_call | solution.py:192
  252.7 1.9 collective-permute-start.4
  254.7 7.3 %reshape.195 = f32[16,4,5,4,8,4]{5,4,3,1,0,2:T(8,128)} reshape(f32[64,5,128]{2,0,1:T(8,128)S(1)} %copy.159) | data formatting | bytes 327680 | tf_op jit(solution)/shard_map/reshape | solution.py:46
  262.0 7.9 %copy.160 = f32[8,16,4,4,4,5]{1,0,4,3,2,5:T(8,128)} copy(f32[8,16,4,4,4,5]{3,0,2,4,1,5:T(8,128)} %bitcast.106) | data formatting | bytes 327680 | tf_op jit(solution)/shard_map/transpose | solution.py:47
  272.6 2.0 reshape.265
  274.6 9.4 %all-to-all-start.3 = ((f32[128,1,320]{2,1,0:T(1,128)}), f32[128,1,320]{2,1,0:T(1,128)S(1)}, u32[]{:S(2)}, u32[]{:S(2)}) async-start(f32[128,1,320]{2,1,0:T(1,128)} %reshape.265), calls=%async_computation.3 | async-start | bytes 393216 | tf_op jit(solution)/shard_map/all_to_all | solution.py:223
  283.9 2.8 multiply_reduce_fusion.3
  286.7 7.0 %collective-permute-start.5 = (f32[96,5,32]{2,1,0:T(8,128)}, f32[96,5,32]{2,1,0:T(8,128)}, u32[]{:S(2)}, u32[]{:S(2)}) collective-permute-start(f32[96,5,32]{2,1,0:T(8,128)} %get-tuple-element.26), channel_id=1, source_target_pairs={{1,0},{2,1},{3,2},{4,3},{5,4},{6,5},{7,6},{8,7},{9,8},{10,9},{11,1... | collective-permute-start | bytes 184328 | tf_op jit(solution)/shard_map/ppermute | solution.py:150
  298.0 1.8 reshape.266
  300.9 7.7 %reshape.197 = f32[512,4,4,5]{2,1,0,3:T(4,128)} reshape(f32[128,64,5]{1,0,2:T(8,128)S(1)} %copy.162) | data formatting | bytes 327680 | tf_op jit(solution)/shard_map/reshape | solution.py:54
  308.6 15.4 %copy.163 = f32[5,4,4,512]{0,3,2,1:T(8,128)} copy(f32[5,4,4,512]{2,1,3,0:T(4,128)} %bitcast.107) | data formatting | bytes 327680 | tf_op jit(solution)/shard_map/transpose | solution.py:55
  324.0 3.7 gather_fusion.2
  332.9 5.7 %all-to-all-start.4 = ((f32[5,128,2]{0,2,1:T(2,128)}), f32[5,128,2]{0,2,1:T(2,128)}, u32[]{:S(2)}, u32[]{:S(2)}) async-start(f32[5,128,2]{0,2,1:T(2,128)} %broadcast_select_fusion), calls=%async_computation.4 | async-start | bytes 262144 | tf_op jit(solution)/shard_map/all_to_all | solution.py:26
  339.5 9.0 %all-to-all-done.4 = f32[5,128,2]{0,2,1:T(2,128)} async-done(((f32[5,128,2]{0,2,1:T(2,128)}), f32[5,128,2]{0,2,1:T(2,128)}, u32[]{:S(2)}, u32[]{:S(2)}) %all-to-all-start.4) | async-done | bytes 5152 | tf_op jit(solution)/shard_map/all_to_all | solution.py:26
  348.5 4.0 scatter_custom_fusion.1
  352.5 3.0 copy.166
  356.2 4.6 copy.167
  360.8 7.0 %reshape.200 = f32[128,64,5]{1,0,2:T(8,128)S(1)} reshape(f32[512,4,4,5]{2,1,0,3:T(4,128)} %copy.167) | data formatting | bytes 327680 | tf_op jit(solution)/shard_map/reshape | solution.py:34
  368.8 2.0 reshape.267
  370.8 4.2 all-to-all-start.5
  377.5 8.2 %all-to-all-done.5 = f32[128,1,320]{2,1,0:T(1,128)S(1)} async-done(((f32[128,1,320]{2,1,0:T(1,128)}), f32[128,1,320]{2,1,0:T(1,128)S(1)}, u32[]{:S(2)}, u32[]{:S(2)}) %all-to-all-start.5) | async-done | bytes 163872 | tf_op jit(solution)/shard_map/all_to_all | solution.py:218
  392.0 7.4 %copy.185 = f32[16,4,5,4,8,4]{5,4,3,2,1,0:T(8,128)} copy(f32[16,4,5,4,8,4]{0,4,1,5,3,2:T(8,128)} %bitcast.120) | data formatting | bytes 327680 | tf_op jit(solution)/shard_map/reshape | solution.py:41
  399.4 5.6 %reshape.258 = f32[64,5,128]{2,1,0:T(8,128)S(1)} reshape(f32[16,4,5,4,8,4]{5,4,3,2,1,0:T(8,128)} %copy.185) | data formatting | bytes 327680 | tf_op jit(solution)/shard_map/reshape | solution.py:41
  408.1 11.5 %shard_map.95 = f32[96,8,128]{2,1,0:T(8,128)} custom-call(f32[96,8,128]{2,1,0:T(8,128)} %copy_subtract_fusion.2.rhs_ref, f32[96,5,8,128]{3,2,1,0:T(8,128)} %pad.85.kx_ref, f32[96,5,8,128]{3,2,1,0:T(8,128)} %pad.93.ky_ref, f32[96,5,8,128]{3,2,1,0:T(8,128)} %pad.94.inv_ref), custom_call_target="tpu_custom_call" | custom-call | tf_op jit(solution)/shard_map/pallas_call | solution.py:192
  421.8 2.3 collective-permute-start.6
  424.1 6.6 %collective-permute-start.7 = (f32[96,5,32]{2,1,0:T(8,128)S(1)}, f32[96,5,32]{2,1,0:T(8,128)S(1)}, u32[]{:S(2)}, u32[]{:S(2)}) collective-permute-start(f32[96,5,32]{2,1,0:T(8,128)S(1)} %get-tuple-element.22), channel_id=1, source_target_pairs={{1,0},{2,1},{3,2},{4,3},{5,4},{6,5},{7,6},{8,7},{9,8},{10,9},{11,1... | collective-permute-start | bytes 184328 | tf_op jit(solution)/shard_map/ppermute | solution.py:150
  431.3 6.8 %collective-permute-done.6 = f32[96,5,32]{2,1,0:T(8,128)S(1)} collective-permute-done((f32[96,5,32]{2,1,0:T(8,128)S(1)}, f32[96,5,32]{2,1,0:T(8,128)S(1)}, u32[]{:S(2)}, u32[]{:S(2)}) %collective-permute-start.6) | collective-permute-done | bytes 61472 | tf_op jit(solution)/shard_map/ppermute | solution.py:153
  440.7 11.7 %shard_map.96 = f32[96,8,128]{2,1,0:T(8,128)} custom-call(f32[96,8,128]{2,1,0:T(8,128)} %copy_subtract_fusion.rhs_ref, f32[96,5,8,128]{3,2,1,0:T(8,128)} %get-tuple-element.19.kx_ref, f32[96,5,8,128]{3,2,1,0:T(8,128)} %get-tuple-element.17.ky_ref, f32[96,5,8,128]{3,2,1,0:T(8,128)} %pad.94.inv_ref), custom_call_target="tpu_custom_call" | custom-call | tf_op jit(solution)/shard_map/pallas_call | solution.py:192
  455.5 6.9 %reshape.203 = f32[16,4,5,4,8,4]{5,4,3,1,0,2:T(8,128)} reshape(f32[64,5,128]{2,0,1:T(8,128)S(1)} %copy.180) | data formatting | bytes 327680 | tf_op jit(solution)/shard_map/reshape | solution.py:46
  462.5 7.3 %copy.181 = f32[8,16,4,4,4,5]{1,0,4,3,2,5:T(8,128)S(1)} copy(f32[8,16,4,4,4,5]{3,0,2,4,1,5:T(8,128)} %bitcast.108) | data formatting | bytes 327680 | tf_op jit(solution)/shard_map/transpose | solution.py:47
  470.7 19.4 %all_to_all.43 = f32[128,1,320]{2,1,0:T(1,128)S(1)} all-to-all(f32[128,1,320]{2,1,0:T(1,128)S(1)} %reshape.269), channel_id=1, replica_groups=mesh['bx'=8,'by'=16] {'bx','by'}, dimensions={0} | all-to-all | bytes 327680 | tf_op jit(solution)/shard_map/all_to_all | solution.py:223
  491.4 7.7 %reshape.205 = f32[512,4,4,5]{2,1,0,3:T(4,128)} reshape(f32[128,64,5]{1,0,2:T(8,128)S(1)} %copy.183) | data formatting | bytes 327680 | tf_op jit(solution)/shard_map/reshape | solution.py:54
  499.1 4.8 copy.184
  (246 shorter events, 80.2 us)
Async XLA Ops:
  1.9 4.4 copy-start.39
  2.7 8.4 %copy-start.30 = (pred[128,2]{1,0:T(8,128)(4,1)}, pred[128,2]{1,0:T(8,128)(4,1)S(1)}, u32[]{:S(2)}) copy-start(pred[128,2]{1,0:T(8,128)(4,1)S(1)} %fusion.17) | copy-start | bytes 772
  2.7 20.8 %copy-start.26 = (f32[5,5,4,4,512]{4,3,2,1,0:T(4,128)S(1)}, f32[5,5,4,4,512]{4,3,2,1,0:T(4,128)}, u32[]{:S(2)}) copy-start(f32[5,5,4,4,512]{4,3,2,1,0:T(4,128)} %param.13) | copy-start | bytes 2457604
  6.3 17.2 %copy-start.17 = (bf16[6,5,5,4,4,512]{5,4,3,2,1,0:T(4,128)(2,1)S(1)}, bf16[6,5,5,4,4,512]{5,4,3,2,1,0:T(4,128)(2,1)}, u32[]{:S(2)}) copy-start(bf16[6,5,5,4,4,512]{5,4,3,2,1,0:T(4,128)(2,1)} %param.14) | copy-start | bytes 7372804
  12.0 21.5 %all-to-all-start = ((f32[5,128,2]{0,2,1:T(2,128)}), f32[5,128,2]{0,2,1:T(2,128)S(1)}, u32[]{:S(2)}, u32[]{:S(2)}) async-start(f32[5,128,2]{0,2,1:T(2,128)} %broadcast_select_fusion.1), calls=%async_computation | async-start | bytes 262144 | tf_op jit(solution)/shard_map/all_to_all | solution.py:26
  33.5 7.3 %copy-start.43 = (s32[4]{0:T(128)S(1)}, s32[4]{0:T(128)}, u32[]{:S(2)}) copy-start(s32[4]{0:T(128)} %constant.194) | copy-start | bytes 52
  33.5 59.7 %all-to-all-start.2 = ((f32[128,64,75]{2,1,0:T(8,128)}), f32[128,64,75]{2,1,0:T(8,128)}, u32[]{:S(2)}, u32[]{:S(2)}) async-start(f32[128,64,75]{2,1,0:T(8,128)} %bitcast.110), calls=%async_computation.2 | async-start | bytes 8388608 | tf_op jit(solution)/shard_map/all_to_all | solution.py:218
  45.0 0.7 copy-start.41
  45.7 3.6 copy-start.42
  93.2 57.2 %all-to-all-start.1 = ((f32[128,64,110]{2,1,0:T(8,128)}), f32[128,64,110]{2,1,0:T(8,128)}, u32[]{:S(2)}, u32[]{:S(2)}) async-start(f32[128,64,110]{2,1,0:T(8,128)} %bitcast.115), calls=%async_computation.1 | async-start | bytes 8388608 | tf_op jit(solution)/shard_map/all_to_all | solution.py:218
  98.2 151.2 %copy-start.32 = (s32[128]{0:T(128)}, s32[128]{0:T(128)S(1)}, u32[]{:S(2)}) copy-start(s32[128]{0:T(128)S(1)} %broadcast_add_fusion) | copy-start | bytes 1540
  98.2 151.1 %copy-start.34 = (s32[128]{0:T(128)}, s32[128]{0:T(128)S(1)}, u32[]{:S(2)}) copy-start(s32[128]{0:T(128)S(1)} %iota_and_fusion) | copy-start | bytes 1540
  98.3 151.1 %copy-start.36 = (pred[128]{0:T(512)(128)(4,1)}, pred[128]{0:T(512)(128)(4,1)S(1)}, u32[]{:S(2)}) copy-start(pred[128]{0:T(512)(128)(4,1)S(1)} %compare_and_fusion.1) | copy-start | bytes 388
  98.3 151.2 %copy-start.28 = (pred[96,5,128]{2,1,0:T(8,128)(4,1)}, pred[96,5,128]{2,1,0:T(8,128)(4,1)S(1)}, u32[]{:S(2)}) copy-start(pred[96,5,128]{2,1,0:T(8,128)(4,1)S(1)} %fusion.12) | copy-start | bytes 184324
  98.4 118.6 %copy-start.24 = (pred[96,8,128]{2,1,0:T(8,128)(4,1)}, pred[96,8,128]{2,1,0:T(8,128)(4,1)S(1)}, u32[]{:S(2)}) copy-start(pred[96,8,128]{2,1,0:T(8,128)(4,1)S(1)} %get-tuple-element.35) | copy-start | bytes 294916
  130.5 2.0 copy-start
  177.9 22.4 %copy-start.15 = (f32[96,5,128]{2,1,0:T(8,128)}, f32[96,5,128]{2,1,0:T(8,128)S(1)}, u32[]{:S(2)}) copy-start(f32[96,5,128]{2,1,0:T(8,128)S(1)} %get-tuple-element.6) | copy-start | bytes 737284
  182.4 17.2 %collective-permute-start = (f32[96,5,32]{2,1,0:T(8,128)S(1)}, f32[96,5,32]{2,1,0:T(8,128)S(1)}, u32[]{:S(2)}, u32[]{:S(2)}) collective-permute-start(f32[96,5,32]{2,1,0:T(8,128)S(1)} %get-tuple-element.12), channel_id=1, source_target_pairs={{0,1},{1,2},{2,3},{3,4},{4,5},{5,6},{6,7},{7,8},{8,9},{9,10},{10,1... | collective-permute-start | bytes 184328 | tf_op jit(solution)/shard_map/ppermute | solution.py:153
  184.5 15.3 %collective-permute-start.1 = (f32[96,5,32]{2,1,0:T(8,128)S(1)}, f32[96,5,32]{2,1,0:T(8,128)S(1)}, u32[]{:S(2)}, u32[]{:S(2)}) collective-permute-start(f32[96,5,32]{2,1,0:T(8,128)S(1)} %get-tuple-element.13), channel_id=1, source_target_pairs={{1,0},{2,1},{3,2},{4,3},{5,4},{6,5},{7,6},{8,7},{9,8},{10,9},{11,1... | collective-permute-start | bytes 184328 | tf_op jit(solution)/shard_map/ppermute | solution.py:150
  192.8 3.5 copy-start.8
  194.3 2.0 copy-start.9
  198.8 1.2 copy-start.3
  213.0 1.2 copy-start.12
  214.6 2.6 copy-start.1
  214.9 16.4 %collective-permute-start.2 = (f32[96,5,32]{2,1,0:T(8,128)S(1)}, f32[96,5,32]{2,1,0:T(8,128)S(1)}, u32[]{:S(2)}, u32[]{:S(2)}) collective-permute-start(f32[96,5,32]{2,1,0:T(8,128)S(1)} %get-tuple-element.29), channel_id=1, source_target_pairs={{0,1},{1,2},{2,3},{3,4},{4,5},{5,6},{6,7},{7,8},{8,9},{9,10},{10,1... | collective-permute-start | bytes 184328 | tf_op jit(solution)/shard_map/ppermute | solution.py:153
  217.5 14.2 %collective-permute-start.3 = (f32[96,5,32]{2,1,0:T(8,128)S(1)}, f32[96,5,32]{2,1,0:T(8,128)S(1)}, u32[]{:S(2)}, u32[]{:S(2)}) collective-permute-start(f32[96,5,32]{2,1,0:T(8,128)S(1)} %get-tuple-element.30), channel_id=1, source_target_pairs={{1,0},{2,1},{3,2},{4,3},{5,4},{6,5},{7,6},{8,7},{9,8},{10,9},{11,1... | collective-permute-start | bytes 184328 | tf_op jit(solution)/shard_map/ppermute | solution.py:150
  231.6 1.3 copy-start.4
  231.7 1.3 copy-start.16
  245.7 1.3 copy-start.7
  249.3 1.5 copy-start.10
  252.7 40.9 %collective-permute-start.4 = (f32[96,5,32]{2,1,0:T(8,128)}, f32[96,5,32]{2,1,0:T(8,128)}, u32[]{:S(2)}, u32[]{:S(2)}) collective-permute-start(f32[96,5,32]{2,1,0:T(8,128)} %get-tuple-element.25), channel_id=1, source_target_pairs={{0,1},{1,2},{2,3},{3,4},{4,5},{5,6},{6,7},{7,8},{8,9},{9,10},{10,1... | collective-permute-start | bytes 184328 | tf_op jit(solution)/shard_map/ppermute | solution.py:153
  274.6 21.0 %all-to-all-start.3 = ((f32[128,1,320]{2,1,0:T(1,128)}), f32[128,1,320]{2,1,0:T(1,128)S(1)}, u32[]{:S(2)}, u32[]{:S(2)}) async-start(f32[128,1,320]{2,1,0:T(1,128)} %reshape.265), calls=%async_computation.3 | async-start | bytes 393216 | tf_op jit(solution)/shard_map/all_to_all | solution.py:223
  283.9 9.7 %copy-start.22 = (f32[96,8,96]{2,1,0:T(8,128)S(1)}, f32[96,8,96]{2,1,0:T(8,128)}, u32[]{:S(2)}) copy-start(f32[96,8,96]{2,1,0:T(8,128)} %get-tuple-element.27) | copy-start | bytes 884740
  286.7 88.4 %collective-permute-start.5 = (f32[96,5,32]{2,1,0:T(8,128)}, f32[96,5,32]{2,1,0:T(8,128)}, u32[]{:S(2)}, u32[]{:S(2)}) collective-permute-start(f32[96,5,32]{2,1,0:T(8,128)} %get-tuple-element.26), channel_id=1, source_target_pairs={{1,0},{2,1},{3,2},{4,3},{5,4},{6,5},{7,6},{8,7},{9,8},{10,9},{11,1... | collective-permute-start | bytes 184328 | tf_op jit(solution)/shard_map/ppermute | solution.py:150
  308.6 19.1 %copy-start.40 = (pred[256]{0:T(512)(128)(4,1)S(1)}, pred[256]{0:T(512)(128)(4,1)}, u32[]{:S(2)}) copy-start(pred[256]{0:T(512)(128)(4,1)} %compare_and_fusion) | copy-start | bytes 772
  308.6 21.7 %copy-start.38 = (f32[1,5,5,256]{3,0,2,1:T(1,128)S(1)}, f32[1,5,5,256]{3,0,2,1:T(1,128)}, u32[]{:S(2)}) copy-start(f32[1,5,5,256]{3,0,2,1:T(1,128)} %param.15) | copy-start | bytes 76804
  308.6 22.5 %copy-start.31 = (pred[128,2]{1,0:T(8,128)(4,1)S(1)}, pred[128,2]{1,0:T(8,128)(4,1)}, u32[]{:S(2)}) copy-start(pred[128,2]{1,0:T(8,128)(4,1)} %copy-done.30) | copy-start | bytes 772
  308.6 30.0 %copy-start.23 = (f32[96,5,128]{2,0,1:T(8,128)S(1)}, f32[96,5,128]{2,0,1:T(8,128)}, u32[]{:S(2)}) copy-start(f32[96,5,128]{2,0,1:T(8,128)} %copy.172) | copy-start | bytes 737284
  332.9 15.6 %all-to-all-start.4 = ((f32[5,128,2]{0,2,1:T(2,128)}), f32[5,128,2]{0,2,1:T(2,128)}, u32[]{:S(2)}, u32[]{:S(2)}) async-start(f32[5,128,2]{0,2,1:T(2,128)} %broadcast_select_fusion), calls=%async_computation.4 | async-start | bytes 262144 | tf_op jit(solution)/shard_map/all_to_all | solution.py:26
  352.5 3.0 copy-start.27
  370.8 14.8 %all-to-all-start.5 = ((f32[128,1,320]{2,1,0:T(1,128)}), f32[128,1,320]{2,1,0:T(1,128)S(1)}, u32[]{:S(2)}, u32[]{:S(2)}) async-start(f32[128,1,320]{2,1,0:T(1,128)} %reshape.267), calls=%async_computation.5 | async-start | bytes 393216 | tf_op jit(solution)/shard_map/all_to_all | solution.py:218
  375.1 1.5 copy-start.5
  399.4 5.7 %copy-start.33 = (s32[128]{0:T(128)S(1)}, s32[128]{0:T(128)}, u32[]{:S(2)}) copy-start(s32[128]{0:T(128)} %copy-done.32) | copy-start | bytes 1540
  399.4 5.7 %copy-start.35 = (s32[128]{0:T(128)S(1)}, s32[128]{0:T(128)}, u32[]{:S(2)}) copy-start(s32[128]{0:T(128)} %copy-done.34) | copy-start | bytes 1540
  399.4 5.7 %copy-start.37 = (pred[128]{0:T(512)(128)(4,1)S(1)}, pred[128]{0:T(512)(128)(4,1)}, u32[]{:S(2)}) copy-start(pred[128]{0:T(512)(128)(4,1)} %copy-done.36) | copy-start | bytes 388
  405.3 1.0 copy-start.18
  405.3 1.1 copy-start.19
  405.4 1.4 copy-start.20
  405.4 1.5 copy-start.21
  405.6 0.7 copy-start.13
  419.6 1.2 copy-start.11
  420.7 0.9 copy-start.25
  420.8 9.9 %copy-start.2 = (f32[96,5,5,128]{3,2,1,0:T(8,128)S(1)}, f32[96,5,5,128]{3,2,1,0:T(8,128)}, u32[]{:S(2)}) copy-start(f32[96,5,5,128]{3,2,1,0:T(8,128)} %copy-done) | copy-start | bytes 3686404
  421.8 16.3 %collective-permute-start.6 = (f32[96,5,32]{2,1,0:T(8,128)S(1)}, f32[96,5,32]{2,1,0:T(8,128)S(1)}, u32[]{:S(2)}, u32[]{:S(2)}) collective-permute-start(f32[96,5,32]{2,1,0:T(8,128)S(1)} %get-tuple-element.21), channel_id=1, source_target_pairs={{0,1},{1,2},{2,3},{3,4},{4,5},{5,6},{6,7},{7,8},{8,9},{9,10},{10,1... | collective-permute-start | bytes 184328 | tf_op jit(solution)/shard_map/ppermute | solution.py:153
  424.1 14.1 %collective-permute-start.7 = (f32[96,5,32]{2,1,0:T(8,128)S(1)}, f32[96,5,32]{2,1,0:T(8,128)S(1)}, u32[]{:S(2)}, u32[]{:S(2)}) collective-permute-start(f32[96,5,32]{2,1,0:T(8,128)S(1)} %get-tuple-element.22), channel_id=1, source_target_pairs={{1,0},{2,1},{3,2},{4,3},{5,4},{6,5},{7,6},{8,7},{9,8},{10,9},{11,1... | collective-permute-start | bytes 184328 | tf_op jit(solution)/shard_map/ppermute | solution.py:150
  431.3 7.1 %copy-start.6 = (f32[96,25,128]{2,0,1:T(8,128)S(1)}, f32[96,25,128]{2,0,1:T(8,128)}, u32[]{:S(2)}) copy-start(f32[96,25,128]{2,0,1:T(8,128)} %copy-done.3) | copy-start | bytes 3686404
  438.5 1.0 copy-start.14
  454.6 0.9 copy-start.29
